TPU v7x, 128 devices: a whole 4x4x4 slice. The times are simulated.
128 devices in a mesh: dp: 32 (over x, y, core), tensor: 4 (over z).
Axes of the slice: x: 4, y: 4, z: 4, core: 2. Of those that a mesh axis runs over, the one named last changes fastest.
Arguments:
- query: bfloat16 [32768, 5120], P('dp', 'tensor'), may hold values from -6 to 6
- keys: bfloat16 [32768, 1024], P('dp', 'tensor'), may hold values from -6 to 6
- values: bfloat16 [32768, 1024], P('dp', 'tensor'), may hold values from -6 to 6
- out_weight: bfloat16 [5120, 2560], P('tensor', 'dp'), may hold values from -0.078125 to 0.078125
- loss_grad: bfloat16 [32768, 2560], P('dp', 'tensor'), may hold values from -6 to 6
- lengths: int32 [32, 16], P('dp'), may hold values from 1 to 512, 1024 in all within a row
- languages: int32 [32, 16], P('dp'), may hold values from 0 to 28
- labels: int32 [32768], P('dp'), may hold values from -100 to 152063, as said below
Outputs:
- attention_result: bfloat16 [32768, 5120], P('dp', 'tensor')
- query_gradient: bfloat16 [32768, 5120], P('dp', 'tensor')
- key_gradient: bfloat16 [32768, 1024], P('dp', 'tensor')
- value_gradient: bfloat16 [32768, 1024], P('dp', 'tensor')
- projection_gradient: bfloat16 [5120, 2560], P('tensor')
Inputs may be any that keep to these rules, and one draw needn't show every extreme that they name: `labels`: each label is -100, meaning no loss on that token, or a token id below 152064.
All inputs are finite; a program needn't handle non-finite values.
Results may differ from a plain program's by a relative error of at most 0.02.
Values may be sent and summed in bfloat16 or wider, within the bound.
No kernel may reach another device: no remote copies, remote signals or barrier semaphores. Data moves between devices by JAX's collectives and lax.ppermute only.
A program may use at most 192 MiB of HBM per device.

v0:
```python
import math

import jax
import jax.numpy as jnp
from jax import lax
from jax.sharding import PartitionSpec as P

QUERY_HEADS = 40
KEY_VALUE_HEADS = 8
HEAD_SIZE = 128
LANGS = 29
DOCS = 16


def token_docs(length_row, row_count):
    doc_ends = jnp.cumsum(length_row)
    places = jnp.arange(row_count, dtype=jnp.int32)
    return jnp.sum((places[:, None] >= doc_ends[None, :]).astype(jnp.int32), axis=1)


def masked_scores(query_rows, key_rows, allowed, factor):
    scores = (
        jnp.einsum("rgd,kd->grk", query_rows, key_rows, preferred_element_type=jnp.float32) * factor
    )
    return jnp.where(allowed[None], scores, -1e30)


def block_forward(query_rows, key_rows, value_rows, allowed, factor):
    scores = masked_scores(query_rows, key_rows, allowed, factor)
    row_top = jnp.max(scores, axis=2, keepdims=True)
    log_total = row_top + jnp.log(jnp.sum(jnp.exp(scores - row_top), axis=2, keepdims=True))
    weights = jnp.exp(scores - log_total).astype(jnp.bfloat16)
    result = jnp.einsum("grk,kd->rgd", weights, value_rows, preferred_element_type=jnp.float32)
    return (result.astype(jnp.bfloat16), log_total[:, :, 0])


def block_backward(
    query_rows, key_rows, value_rows, allowed, out_rows, log_rows, grad_rows, factor
):
    scores = masked_scores(query_rows, key_rows, allowed, factor)
    weights = jnp.exp(scores - log_rows[:, :, None])
    value_gradient = jnp.einsum(
        "grk,rgd->kd", weights.astype(jnp.bfloat16), grad_rows, preferred_element_type=jnp.float32
    )
    weight_grad = jnp.einsum(
        "rgd,kd->grk", grad_rows, value_rows, preferred_element_type=jnp.float32
    )
    diagonal_term = jnp.einsum(
        "rgd,rgd->gr", grad_rows, out_rows, preferred_element_type=jnp.float32
    )
    score_grad = (weights * (weight_grad - diagonal_term[:, :, None]) * factor).astype(jnp.bfloat16)
    query_gradient = jnp.einsum(
        "grk,kd->rgd", score_grad, key_rows, preferred_element_type=jnp.float32
    )
    key_gradient = jnp.einsum(
        "grk,rgd->kd", score_grad, query_rows, preferred_element_type=jnp.float32
    )
    return (query_gradient, key_gradient, value_gradient)


def pack_layout(doc_ids):
    row_count = doc_ids.shape[0]
    places = jnp.arange(row_count, dtype=jnp.int32)
    allowed = (doc_ids[:, None] == doc_ids[None, :]) & (places[:, None] >= places[None, :])
    half_rows = row_count // 2
    key_step = row_count // 8
    first_row = jnp.min(jnp.where(doc_ids == doc_ids[half_rows], places, row_count))
    return (allowed, half_rows, key_step, first_row // key_step)


def pack_forward(query, keys, values, doc_ids, factor):
    allowed, half_rows, key_step, bucket = pack_layout(doc_ids)
    row_count = doc_ids.shape[0]
    group_size = QUERY_HEADS // KEY_VALUE_HEADS
    outs = []
    logs = []
    for head_cluster in range(keys.shape[1] // HEAD_SIZE):
        query_part = query[
            :, head_cluster * group_size * HEAD_SIZE : (head_cluster + 1) * group_size * HEAD_SIZE
        ].reshape(row_count, group_size, HEAD_SIZE)
        key_part = keys[:, head_cluster * HEAD_SIZE : (head_cluster + 1) * HEAD_SIZE]
        value_part = values[:, head_cluster * HEAD_SIZE : (head_cluster + 1) * HEAD_SIZE]
        early_out, early_log = block_forward(
            query_part[:half_rows],
            key_part[:half_rows],
            value_part[:half_rows],
            allowed[:half_rows, :half_rows],
            factor,
        )

        def later_block(bucket_id):
            first_key = bucket_id * key_step

            def run_block(operands):
                query_late, key_all, value_all = operands
                return block_forward(
                    query_late,
                    key_all[first_key:],
                    value_all[first_key:],
                    allowed[half_rows:, first_key:],
                    factor,
                )

            return run_block

        late_out, late_log = lax.switch(
            bucket,
            [later_block(bucket_id) for bucket_id in range(5)],
            (query_part[half_rows:], key_part, value_part),
        )
        outs.append(
            jnp.concatenate([early_out, late_out], axis=0).reshape(
                row_count, group_size * HEAD_SIZE
            )
        )
        logs.append(jnp.concatenate([early_log, late_log], axis=1))
    return (jnp.concatenate(outs, axis=1), jnp.stack(logs, axis=0))


def pack_backward(query, keys, values, doc_ids, attn_rows, log_rows, grad_rows, factor):
    allowed, half_rows, key_step, bucket = pack_layout(doc_ids)
    row_count = doc_ids.shape[0]
    group_size = QUERY_HEADS // KEY_VALUE_HEADS
    query_parts = []
    key_parts = []
    value_parts = []
    for head_cluster in range(keys.shape[1] // HEAD_SIZE):
        span = slice(
            head_cluster * group_size * HEAD_SIZE, (head_cluster + 1) * group_size * HEAD_SIZE
        )
        query_part = query[:, span].reshape(row_count, group_size, HEAD_SIZE)
        attn_part = attn_rows[:, span].reshape(row_count, group_size, HEAD_SIZE)
        grad_part = grad_rows[:, span].reshape(row_count, group_size, HEAD_SIZE)
        key_part = keys[:, head_cluster * HEAD_SIZE : (head_cluster + 1) * HEAD_SIZE]
        value_part = values[:, head_cluster * HEAD_SIZE : (head_cluster + 1) * HEAD_SIZE]
        log_part = log_rows[head_cluster]
        early_query, early_key, early_value = block_backward(
            query_part[:half_rows],
            key_part[:half_rows],
            value_part[:half_rows],
            allowed[:half_rows, :half_rows],
            attn_part[:half_rows],
            log_part[:, :half_rows],
            grad_part[:half_rows],
            factor,
        )

        def later_block(bucket_id):
            first_key = bucket_id * key_step

            def run_block(operands):
                query_late, key_all, value_all, attn_late, log_late, grad_late = operands
                late_query, late_key, late_value = block_backward(
                    query_late,
                    key_all[first_key:],
                    value_all[first_key:],
                    allowed[half_rows:, first_key:],
                    attn_late,
                    log_late,
                    grad_late,
                    factor,
                )
                return (
                    late_query,
                    jnp.pad(late_key, ((first_key, 0), (0, 0))),
                    jnp.pad(late_value, ((first_key, 0), (0, 0))),
                )

            return run_block

        late_query, late_key, late_value = lax.switch(
            bucket,
            [later_block(bucket_id) for bucket_id in range(5)],
            (
                query_part[half_rows:],
                key_part,
                value_part,
                attn_part[half_rows:],
                log_part[:, half_rows:],
                grad_part[half_rows:],
            ),
        )
        tail_rows = row_count - half_rows
        key_total = late_key + jnp.pad(early_key, ((0, tail_rows), (0, 0)))
        value_total = late_value + jnp.pad(early_value, ((0, tail_rows), (0, 0)))
        query_parts.append(
            jnp.concatenate([early_query, late_query], axis=0)
            .astype(jnp.bfloat16)
            .reshape(row_count, group_size * HEAD_SIZE)
        )
        key_parts.append(key_total.astype(jnp.bfloat16))
        value_parts.append(value_total.astype(jnp.bfloat16))
    return (
        jnp.concatenate(query_parts, axis=1),
        jnp.concatenate(key_parts, axis=1),
        jnp.concatenate(value_parts, axis=1),
    )


def shards(query, keys, values, out_weight, loss_grad, lengths, languages, labels):
    factor = 1.0 / math.sqrt(HEAD_SIZE)
    row_count = query.shape[0]
    doc_ids = token_docs(lengths[0], row_count)
    attention_result, log_rows = pack_forward(query, keys, values, doc_ids, factor)
    token_lang = jnp.sum(
        jnp.where(
            doc_ids[:, None] == jnp.arange(DOCS, dtype=jnp.int32)[None, :], languages[0][None, :], 0
        ),
        axis=1,
    )
    counted = labels != -100
    lang_match = token_lang[:, None] == jnp.arange(LANGS, dtype=jnp.int32)[None, :]
    local_counts = jnp.sum((lang_match & counted[:, None]).astype(jnp.int32), axis=0)
    counts = lax.psum(local_counts, "dp").astype(jnp.float32)
    lang_weight = jnp.sqrt(jnp.sum(counts) / (LANGS * jnp.maximum(counts, 1.0)))
    token_weight = jnp.where(
        counted, jnp.sum(jnp.where(lang_match, lang_weight[None, :], 0.0), axis=1), 0.0
    )
    full_grad = lax.all_gather(loss_grad, "tensor", axis=1, tiled=True)
    weighted = (token_weight[:, None] * full_grad.astype(jnp.float32)).astype(jnp.bfloat16)
    out_grad = lax.dot_general(
        weighted,
        lax.all_gather(out_weight, "dp", axis=1, tiled=True),
        (((1,), (1,)), ((), ())),
        preferred_element_type=jnp.float32,
    ).astype(jnp.bfloat16)
    local_term = lax.dot_general(
        attention_result, weighted, (((0,), (0,)), ((), ())), preferred_element_type=jnp.float32
    )
    projection_gradient = lax.psum(local_term, "dp").astype(jnp.bfloat16)
    query_gradient, key_gradient, value_gradient = pack_backward(
        query, keys, values, doc_ids, attention_result, log_rows, out_grad, factor
    )
    return (attention_result, query_gradient, key_gradient, value_gradient, projection_gradient)


def solution(mesh):
    in_specs = (
        P("dp", "tensor"),
        P("dp", "tensor"),
        P("dp", "tensor"),
        P("tensor", "dp"),
        P("dp", "tensor"),
        P("dp", None),
        P("dp", None),
        P("dp"),
    )
    out_specs = (
        P("dp", "tensor"),
        P("dp", "tensor"),
        P("dp", "tensor"),
        P("dp", "tensor"),
        P("tensor", None),
    )
    return jax.shard_map(shards, mesh=mesh, in_specs=in_specs, out_specs=out_specs, check_vma=False)
```

profile of v0, /device:TPU:0, one launch (start us, length us, event | category | flops | bytes accessed | tf_op | source)
XLA Modules:
  0.0 488.8 jit_solution(5193281116214088222)
XLA Ops:
  14.7 3.4 fusion.356
  25.2 19.4 %conditional.9 = (f32[5,512]{1,0:T(8,128)}, bf16[512,5,128]{2,0,1:T(8,128)(2,1)}) conditional(s32[]{:T(128)} %clamp.2, (pred[1024,1024]{0,1:T(8,128)(4,1)S(1)}, bf16[1024,128]{1,0:T(8,128)(2,1)}, bf16[512,5,128]{0,2,1:T(8,128)(2,1)}, bf16[1024,128]{1,0:T(8,128)(2,1)}) %tuple.143, (pred[1024,1024]{0,1:T(8,128)(4,1)S(1)}, ...), branch_computations={%region_22.25_spmd, %region_25.28_spmd, %region_28.31_spmd, %regio... | conditional | flops 1371338240 | bytes 35985424
  40.2 3.6 fusion.108
  44.7 15.9 %conditional.8 = (f32[5,512]{1,0:T(8,128)}, bf16[512,5,128]{2,0,1:T(8,128)(2,1)}) conditional(s32[]{:T(128)} %clamp.2, (pred[1024,1024]{0,1:T(8,128)(4,1)S(1)}, bf16[1024,128]{1,0:T(8,128)(2,1)S(1)}, bf16[512,5,128]{0,2,1:T(8,128)(2,1)S(1)}, bf16[1024,128]{1,0:T(8,128)(2,1)S(1)}) %tuple.288, ...), branch_computations={%region_5.8_spmd, %region_8.11_spmd, %region_11.14_spmd, %region_1... | conditional | flops 1371338240 | bytes 35985424
  56.9 3.4 fusion.50
  60.9 28.0 %psum.14 = s32[29]{0:T(128)S(1)} all-reduce(s32[29]{0:T(128)S(1)} %convert_reduce_fusion), channel_id=1, replica_groups=mesh['dp'=32,'tensor'=4] {'dp'}, use_global_device_ids=true, to_apply=%region_39.40 | all-reduce | flops 29 | bytes 232 | tf_op jit(solution)/shard_map/psum | solution.py:214
  92.9 3.3 exponential_reduce_fusion.11
  100.3 20.9 %all-gather.5.cloned.1.call-done = bf16[1280,2560]{0,1:T(8,128)(2,1)} async-done(((bf16[1280,80]{0,1:T(8,128)(2,1)}), bf16[1280,2560]{0,1:T(8,128)(2,1)}) %all-gather.5.cloned.1.call-update) | async-done | bytes 6553616 | tf_op jit(solution)/shard_map/all_gather | solution.py:223
  121.2 11.1 %convolution_convert_fusion.10 = bf16[1024,1280]{1,0:T(8,128)(2,1)S(1)} fusion(bf16[1280,2560]{0,1:T(8,128)(2,1)} %all-gather.5.cloned.1.call-done, bf16[1024,2560]{1,0:T(8,128)(2,1)} %all-gather.3.cloned.1.call-done, f32[1024]{0:T(1024)} %broadcast_select_fusion), kind=kOutput, calls=%fused_computation.399 | convolution fusion | flops 6720061440 | bytes 14422016 | tf_op jit(solution)/shard_map/dot_general | solution.py:221
  138.1 5.5 %multiply_reduce_fusion.10 = (f32[5,512]{1,0:T(8,128)S(1)}, bf16[5,512,128]{2,1,0:T(8,128)(2,1)}) fusion(f32[5,512,128]{2,1,0:T(8,128)} %copy.501, bf16[1024,256]{1,0:T(8,128)(2,1)} %param.30, f32[512,512,5]{1,0,2:T(8,128)} %copy-done.3, f32[5,512]{1,0:T(8,128)} %get-tuple-element.747, pred[512,512]{0,1:T(8,128)(4,1)} %copy-done.24), kind=kOutput, calls=%fused_computation.411 | convolution fusion | flops 342095360 | bytes 7628800 | tf_op jit(solution)/shard_map/grk,kd->rgd/dot_general | solution.py:33
  143.6 4.8 convolution_bitcast_fusion.10
  148.4 4.6 fusion.322
  161.5 5.4 %multiply_reduce_fusion.11 = (f32[5,512]{1,0:T(8,128)S(1)}, bf16[5,512,128]{2,1,0:T(8,128)(2,1)}) fusion(f32[5,512,128]{2,1,0:T(8,128)} %copy.491, bf16[1024,256]{1,0:T(8,128)(2,1)} %param.30, f32[512,512,5]{1,0,2:T(8,128)} %copy-done.2, f32[5,512]{1,0:T(8,128)S(1)} %get-tuple-element.748, pred[512,512]{0,1:T(8,128)(4,1)} %copy-done.24), kind=kOutput, calls=%fused_computation.412 | convolution fusion | flops 342095360 | bytes 7622656 | tf_op jit(solution)/shard_map/grk,kd->rgd/dot_general | solution.py:33
  167.0 4.7 convolution_bitcast_fusion.11
  171.7 4.6 fusion.325
  180.7 43.5 %conditional.11 = (f32[1024,128]{0,1:T(8,128)}, f32[1024,128]{0,1:T(8,128)}, bf16[512,640]{1,0:T(8,128)(2,1)}) conditional(s32[]{:T(128)} %clamp.2, (pred[1024,1024]{0,1:T(8,128)(4,1)S(1)}, bf16[1024,128]{1,0:T(8,128)(2,1)}, bf16[512,5,128]{0,2,1:T(8,128)(2,1)}, f32[5,512]{1,0:T(8,128)}, bf16[1024,128]{1,0:T(8,128)(2,1)}, ...), branch_computations={%region_47.48_spmd, %region_48.49_spmd, %region_49.50_spmd, %regio... | conditional | flops 3385587200 | bytes 70971472 | solution.py:171
  200.7 3.1 multiply_reduce_fusion.9
  206.9 3.1 fusion.308
  210.0 3.0 fusion.301
  212.9 2.8 convolution_bitcast_fusion.9
  224.3 40.6 %conditional.10 = (f32[1024,128]{0,1:T(8,128)S(1)}, f32[1024,128]{0,1:T(8,128)S(1)}, bf16[512,640]{1,0:T(8,128)(2,1)S(1)}) conditional(s32[]{:T(128)} %clamp.2, (pred[1024,1024]{0,1:T(8,128)(4,1)}, bf16[1024,128]{1,0:T(8,128)(2,1)S(1)}, bf16[512,5,128]{0,2,1:T(8,128)(2,1)S(1)}, f32[5,512]{1,0:T(8,128)}, ...), branch_computations={%region_42.43_spmd, %region_43.44_spmd, %region_44.45_spmd, %regio... | conditional | flops 3385587200 | bytes 72020072 | solution.py:171
  260.0 2.7 fusion.199
  284.1 12.7 %fusion.331 = f32[1280,2560]{1,0:T(8,128)} fusion(bf16[1024,2560]{1,0:T(8,128)(2,1)} %all-gather.3.cloned.1.call-done, f32[1024]{0:T(1024)S(1)} %copy-done.51, bf16[1024,640]{0,1:T(8,128)(2,1)} %bitcast.875, bf16[1024,640]{0,1:T(8,128)(2,1)} %bitcast.877), kind=kOutput, calls=%fused_computation.404 | convolution fusion | flops 6723993600 | bytes 20975616 | tf_op jit(solution)/shard_map/dot_general | solution.py:227
  296.8 183.2 %all-reduce.21 = bf16[1280,2560]{1,0:T(8,128)(2,1)} all-reduce(f32[1280,2560]{1,0:T(8,128)} %fusion.331), channel_id=1, replica_groups=mesh['dp'=32,'tensor'=4] {'dp'}, use_global_device_ids=true, to_apply=%region_52.53 | all-reduce | flops 3276800 | bytes 19660800 | tf_op jit(solution)/shard_map/psum | solution.py:230
  (151 shorter events, 100.6 us)
Async XLA Ops:
  7.2 93.1 %all-gather.3.cloned.1.call-start = ((), (), s32[]{:S(2)}) async-start(), calls=%async_computation | async-start | bytes 6553600 | tf_op jit(solution)/shard_map/all_gather | solution.py:219
  7.9 113.3 %all-gather.5.cloned.1.call-start = ((), (), s32[]{:S(2)}) async-start(), calls=%async_computation.1 | async-start | bytes 6758400 | tf_op jit(solution)/shard_map/all_gather | solution.py:223
  14.6 30.1 %copy-start = (pred[1024,1024]{0,1:T(8,128)(4,1)}, pred[1024,1024]{0,1:T(8,128)(4,1)S(1)}, u32[]{:S(2)}) copy-start(pred[1024,1024]{0,1:T(8,128)(4,1)S(1)} %fusion.328) | copy-start | bytes 3145732
  14.7 81.5 %copy-start.24 = (pred[512,512]{0,1:T(8,128)(4,1)}, pred[512,512]{0,1:T(8,128)(4,1)S(1)}, u32[]{:S(2)}) copy-start(pred[512,512]{0,1:T(8,128)(4,1)S(1)} %slice.324) | copy-start | bytes 786436
  22.0 68.9 %copy-start.4 = (bf16[512,640]{0,1:T(8,128)(2,1)}, bf16[512,640]{0,1:T(8,128)(2,1)S(1)}, u32[]{:S(2)}) copy-start(bf16[512,640]{0,1:T(8,128)(2,1)S(1)} %copy.578) | copy-start | bytes 1966084
  25.2 19.5 %copy-start.43 = (bf16[1024,128]{1,0:T(8,128)(2,1)}, bf16[1024,128]{1,0:T(8,128)(2,1)S(1)}, u32[]{:S(2)}) copy-start(bf16[1024,128]{1,0:T(8,128)(2,1)S(1)} %get-tuple-element.734) | copy-start | bytes 786436
  44.7 16.0 %copy-start.52 = (s32[1,16]{1,0:T(1,128)S(1)}, s32[1,16]{1,0:T(1,128)}, u32[]{:S(2)}) copy-start(s32[1,16]{1,0:T(1,128)} %param.34) | copy-start | bytes 196
  44.7 16.1 %copy-start.49 = (s32[1024]{0:T(1024)S(1)}, s32[1024]{0:T(1024)}, u32[]{:S(2)}) copy-start(s32[1024]{0:T(1024)} %param.35) | copy-start | bytes 12292
  60.7 32.2 %copy-start.28 = (bf16[512,640]{0,1:T(8,128)(2,1)S(1)}, bf16[512,640]{0,1:T(8,128)(2,1)}, u32[]{:S(2)}) copy-start(bf16[512,640]{0,1:T(8,128)(2,1)} %copy.580) | copy-start | bytes 1966084
  138.1 5.5 %copy-start.13 = (bf16[512,640]{0,1:T(8,128)(2,1)S(1)}, bf16[512,640]{0,1:T(8,128)(2,1)}, u32[]{:S(2)}) copy-start(bf16[512,640]{0,1:T(8,128)(2,1)} %copy.306) | copy-start | bytes 1966084
  138.1 5.5 %copy-start.25 = (pred[512,512]{0,1:T(8,128)(4,1)S(1)}, pred[512,512]{0,1:T(8,128)(4,1)}, u32[]{:S(2)}) copy-start(pred[512,512]{0,1:T(8,128)(4,1)} %copy-done.24) | copy-start | bytes 786436
  138.1 5.5 %copy-start.50 = (f32[5,512]{1,0:T(8,128)S(1)}, f32[5,512]{1,0:T(8,128)}, u32[]{:S(2)}) copy-start(f32[5,512]{1,0:T(8,128)} %get-tuple-element.747) | copy-start | bytes 30724
  161.5 5.5 %copy-start.12 = (bf16[512,640]{0,1:T(8,128)(2,1)S(1)}, bf16[512,640]{0,1:T(8,128)(2,1)}, u32[]{:S(2)}) copy-start(bf16[512,640]{0,1:T(8,128)(2,1)} %copy.283) | copy-start | bytes 1966084
  161.5 5.5 %copy-start.26 = (pred[512,512]{0,1:T(8,128)(4,1)S(1)}, pred[512,512]{0,1:T(8,128)(4,1)}, u32[]{:S(2)}) copy-start(pred[512,512]{0,1:T(8,128)(4,1)} %copy-done.24) | copy-start | bytes 786436
  171.7 4.6 copy-start.5
  264.9 6.7 %copy-start.8 = (bf16[512,640]{1,0:T(8,128)(2,1)}, bf16[512,640]{1,0:T(8,128)(2,1)S(1)}, u32[]{:S(2)}) copy-start(bf16[512,640]{1,0:T(8,128)(2,1)S(1)} %get-tuple-element.702) | copy-start | bytes 1966084
  265.8 5.8 %copy-start.10 = (bf16[5,512,128]{1,2,0:T(8,128)(2,1)S(1)}, bf16[5,512,128]{1,2,0:T(8,128)(2,1)}, u32[]{:S(2)}) copy-start(bf16[5,512,128]{1,2,0:T(8,128)(2,1)} %convolution_convert_fusion.11) | copy-start | bytes 1966084
  268.7 6.6 %copy-start.11 = (bf16[5,512,128]{1,2,0:T(8,128)(2,1)S(1)}, bf16[5,512,128]{1,2,0:T(8,128)(2,1)}, u32[]{:S(2)}) copy-start(bf16[5,512,128]{1,2,0:T(8,128)(2,1)} %convolution_convert_fusion.12) | copy-start | bytes 1966084
  271.6 4.8 copy-start.30
  271.9 5.5 %copy-start.32 = (f32[1024,128]{0,1:T(8,128)S(1)}, f32[1024,128]{0,1:T(8,128)}, u32[]{:S(2)}) copy-start(f32[1024,128]{0,1:T(8,128)} %copy-done.31) | copy-start | bytes 1572868
  279.5 4.6 copy-start.51
  296.8 183.2 %copy-start.6 = (bf16[512,640]{1,0:T(8,128)(2,1)S(1)}, bf16[512,640]{1,0:T(8,128)(2,1)}, u32[]{:S(2)}) copy-start(bf16[512,640]{1,0:T(8,128)(2,1)} %copy.304) | copy-start | bytes 1966084
  296.8 183.3 %copy-start.7 = (bf16[512,640]{1,0:T(8,128)(2,1)S(1)}, bf16[512,640]{1,0:T(8,128)(2,1)}, u32[]{:S(2)}) copy-start(bf16[512,640]{1,0:T(8,128)(2,1)} %get-tuple-element.705) | copy-start | bytes 1966084
  296.8 183.3 %copy-start.9 = (bf16[512,640]{1,0:T(8,128)(2,1)S(1)}, bf16[512,640]{1,0:T(8,128)(2,1)}, u32[]{:S(2)}) copy-start(bf16[512,640]{1,0:T(8,128)(2,1)} %copy-done.8) | copy-start | bytes 1966084
  (11 other events, 26.9 us)
Sparse Core Ops, SparseCore 0:
  9.7 59.6 all-gather.2
  71.6 49.5 all-gather.4
where the time goes:
time: 496 us; the launch traced here: 489 us
  blocking collectives  211 us (43%)
  matrix products  97.9 us (20%)
  local copies, waits for them, and re-layouts  57.7 us (12%)
  loops' own time  57.1 us (12%)
  other arithmetic  25.3 us (5%)
  waiting for transfers between devices  22.3 us (4%)
  between operations  17.2 us (3%)
    psum x1, blocking collectives, shards(): projection_gradient = lax.psum(local_term, 'dp').astype(jnp.bfloat16)  183 us
    another operation x2, loops' own time, pack_backward(): lax.switch(bucket, [later_block(bucket_id) for bucket_id in range(5)], (q...  35.3 us
    psum x1, blocking collectives, shards(): counts = lax.psum(local_counts, 'dp').astype(jnp.float32)  28 us
    unnamed x2, loops' own time  21.8 us
    all_gather x1, waiting for transfers between devices, shards(): lax.all_gather(out_weight, 'dp', axis=1, tiled=True)  20.9 us
    dot_general x4, matrix products, block_forward(): jnp.einsum('grk,kd->rgd', weights, value_rows, preferred_element_type=jnp...  17.9 us
    unnamed x65, local copies, waits for them, and re-layouts  17.9 us
    dot_general x4, matrix products, block_backward(): jnp.einsum('grk,rgd->kd', weights.astype(jnp.bfloat16), grad_rows, prefer...  15 us
  transfers between devices with their start and end apart: 2, of which 1 were waited for; matrix products, arithmetic and copies ran while one was open for 8% of the time, Pallas kernels for 0%

commit v1 on v0

--- a/solution.py
+++ b/solution.py
@@ -211,7 +211,7 @@
     counted = labels != -100
     lang_match = token_lang[:, None] == jnp.arange(LANGS, dtype=jnp.int32)[None, :]
     local_counts = jnp.sum((lang_match & counted[:, None]).astype(jnp.int32), axis=0)
-    counts = lax.psum(local_counts, "dp").astype(jnp.float32)
+    counts = jnp.sum(lax.all_gather(local_counts, "dp"), axis=0).astype(jnp.float32)
     lang_weight = jnp.sqrt(jnp.sum(counts) / (LANGS * jnp.maximum(counts, 1.0)))
     token_weight = jnp.where(
         counted, jnp.sum(jnp.where(lang_match, lang_weight[None, :], 0.0), axis=1), 0.0
@@ -227,7 +227,10 @@
     local_term = lax.dot_general(
         attention_result, weighted, (((0,), (0,)), ((), ())), preferred_element_type=jnp.float32
     )
-    projection_gradient = lax.psum(local_term, "dp").astype(jnp.bfloat16)
+    projection_part = lax.psum_scatter(local_term, "dp", scatter_dimension=0, tiled=True)
+    projection_gradient = lax.all_gather(
+        projection_part.astype(jnp.bfloat16), "dp", axis=0, tiled=True
+    )
     query_gradient, key_gradient, value_gradient = pack_backward(
         query, keys, values, doc_ids, attention_result, log_rows, out_grad, factor
     )

time: 496 us -> 436 us (0.88)
  the two profiles are of different devices: /device:TPU:0 before, /device:TPU:2 now
where the time goes in v1:
time: 436 us; the launch traced here: 427 us
  waiting for transfers between devices  130 us (30%)
  matrix products  97.7 us (22%)
  local copies, waits for them, and re-layouts  71.2 us (16%)
  loops' own time  69.7 us (16%)
  other arithmetic  25.6 us (6%)
  between operations  17.9 us (4%)
  blocking collectives  15.6 us (4%)
    reduce_scatter x1, waiting for transfers between devices, shards(): lax.psum_scatter(local_term, 'dp', scatter_dimension=0, tiled=True)  105 us
    another operation x2, loops' own time, pack_backward(): lax.switch(bucket, [later_block(bucket_id) for bucket_id in range(5)], (q...  43.6 us
    unnamed x79, local copies, waits for them, and re-layouts  26.9 us
    unnamed x2, loops' own time  26.1 us
    all_gather x1, waiting for transfers between devices, shards(): lax.all_gather(out_weight, 'dp', axis=1, tiled=True)  23.1 us
    dot_general x4, matrix products, block_forward(): jnp.einsum('grk,kd->rgd', weights, value_rows, preferred_element_type=jnp...  16.4 us
    dot_general x4, matrix products, block_backward(): jnp.einsum('rgd,kd->grk', grad_rows, value_rows, preferred_element_type=j...  16 us
    unnamed x1, blocking collectives  15.6 us
  transfers between devices with their start and end apart: 4, of which 2 were waited for; matrix products, arithmetic and copies ran while one was open for 31% of the time, Pallas kernels for 0%

profile of v1, /device:TPU:2, one launch (start us, length us, event | category | flops | bytes accessed | tf_op | source)
XLA Modules:
  0.0 427.4 jit_solution(10076670142648840509)
XLA Ops:
  17.8 15.6 %all-reduce.20 = s32[928]{0:T(1024)S(1)} all-reduce(s32[928]{0:T(1024)S(1)} %dynamic-update-slice), channel_id=2, replica_groups=mesh['dp'=32,'tensor'=4] {'dp'}, use_global_device_ids=true, to_apply=%add.20 | all-reduce | flops 928 | bytes 7424
  34.2 3.4 fusion.356
  45.7 23.9 %conditional.9 = (f32[5,512]{1,0:T(8,128)}, bf16[512,5,128]{2,0,1:T(8,128)(2,1)S(1)}) conditional(s32[]{:T(128)} %clamp.2, (pred[1024,1024]{0,1:T(8,128)(4,1)S(1)}, bf16[1024,128]{1,0:T(8,128)(2,1)}, bf16[512,5,128]{0,2,1:T(8,128)(2,1)}, bf16[1024,128]{1,0:T(8,128)(2,1)}) %tuple.143, ...), branch_computations={%region_22.25_spmd, %region_25.28_spmd, %region_28.31_spmd, %regio... | conditional | flops 1371338240 | bytes 35985424
  69.7 15.7 %conditional.8 = (f32[5,512]{1,0:T(8,128)}, bf16[512,5,128]{2,0,1:T(8,128)(2,1)S(1)}) conditional(s32[]{:T(128)} %clamp.2, (pred[1024,1024]{0,1:T(8,128)(4,1)S(1)}, bf16[1024,128]{1,0:T(8,128)(2,1)S(1)}, bf16[512,5,128]{0,2,1:T(8,128)(2,1)S(1)}, bf16[1024,128]{1,0:T(8,128)(2,1)}) %tuple.294, ...), branch_computations={%region_5.8_spmd, %region_8.11_spmd, %region_11.14_spmd, %region_1... | conditional | flops 1371338240 | bytes 37034028
  89.6 3.3 exponential_reduce_fusion.11
  97.0 23.1 %all-gather.7.cloned.1.call-done = bf16[1280,2560]{0,1:T(8,128)(2,1)} async-done(((bf16[1280,80]{0,1:T(8,128)(2,1)}), bf16[1280,2560]{0,1:T(8,128)(2,1)}) %all-gather.7.cloned.1.call-update) | async-done | bytes 6553616 | tf_op jit(solution)/shard_map/all_gather | solution.py:223
  120.2 11.4 %convolution_convert_fusion.10 = bf16[1024,1280]{1,0:T(8,128)(2,1)S(1)} fusion(bf16[1280,2560]{0,1:T(8,128)(2,1)} %all-gather.7.cloned.1.call-done, bf16[1024,2560]{1,0:T(8,128)(2,1)} %all-gather.5.cloned.1.call-done, f32[1024]{0:T(1024)} %broadcast_select_fusion), kind=kOutput, calls=%fused_computation.399 | convolution fusion | flops 6720061440 | bytes 14422016 | tf_op jit(solution)/shard_map/dot_general | solution.py:221
  141.8 5.3 %multiply_reduce_fusion.10 = (f32[5,512]{1,0:T(8,128)}, bf16[5,512,128]{2,1,0:T(8,128)(2,1)S(1)}) fusion(f32[5,512,128]{2,1,0:T(8,128)} %copy.501, bf16[1024,256]{1,0:T(8,128)(2,1)} %param.30, f32[512,512,5]{1,0,2:T(8,128)} %copy-done.9, f32[5,512]{1,0:T(8,128)} %get-tuple-element.747, pred[512,512]{0,1:T(8,128)(4,1)S(1)} %slice.324), kind=kOutput, calls=%fused_computation.411 | convolution fusion | flops 342095360 | bytes 7628800 | tf_op jit(solution)/shard_map/grk,kd->rgd/dot_general | solution.py:33
  150.8 5.3 %multiply_reduce_fusion.11 = (f32[5,512]{1,0:T(8,128)}, bf16[5,512,128]{2,1,0:T(8,128)(2,1)S(1)}) fusion(f32[5,512,128]{2,1,0:T(8,128)} %copy.491, bf16[1024,256]{1,0:T(8,128)(2,1)} %param.30, f32[512,512,5]{1,0,2:T(8,128)} %copy-done.8, f32[5,512]{1,0:T(8,128)S(1)} %get-tuple-element.748, pred[512,512]{0,1:T(8,128)(4,1)S(1)} %slice.324), kind=kOutput, calls=%fused_computation.412 | convolution fusion | flops 342095360 | bytes 7622656 | tf_op jit(solution)/shard_map/grk,kd->rgd/dot_general | solution.py:33
  159.7 12.8 %fusion.331 = f32[1280,2560]{1,0:T(8,128)} fusion(bf16[1024,2560]{1,0:T(8,128)(2,1)} %all-gather.5.cloned.1.call-done, f32[1024]{0:T(1024)S(1)} %copy-done.61, bf16[1024,640]{0,1:T(8,128)(2,1)} %bitcast.885, bf16[1024,640]{0,1:T(8,128)(2,1)} %bitcast.887), kind=kOutput, calls=%fused_computation.404 | convolution fusion | flops 6723993600 | bytes 20975616 | tf_op jit(solution)/shard_map/dot_general | solution.py:227
  172.6 105.0 %reduce-scatter.2.cloned.1.call-done = f32[40,2560]{1,0:T(8,128)} async-done(((f32[1280,2560]{1,0:T(8,128)}), f32[40,2560]{1,0:T(8,128)}) %reduce-scatter.2.cloned.1.call-update) | async-done | bytes 409616 | tf_op jit(solution)/shard_map/reduce_scatter | solution.py:230
  279.4 51.7 %conditional.11 = (f32[1024,128]{0,1:T(8,128)}, f32[1024,128]{0,1:T(8,128)}, bf16[512,640]{1,0:T(8,128)(2,1)}) conditional(s32[]{:T(128)} %clamp.2, (pred[1024,1024]{0,1:T(8,128)(4,1)}, bf16[1024,128]{1,0:T(8,128)(2,1)}, bf16[512,5,128]{0,2,1:T(8,128)(2,1)}, f32[5,512]{1,0:T(8,128)}, bf16[1024,128]{1,0:T(8,128)(2,1)}, ...), branch_computations={%region_47.48_spmd, %region_48.49_spmd, %region_49.50_spmd, %regio... | conditional | flops 3385587200 | bytes 70971472 | solution.py:171
  299.2 3.1 multiply_reduce_fusion.8
  305.6 3.4 fusion.287
  309.0 3.5 fusion.280
  331.1 45.3 %conditional.10 = (f32[1024,128]{0,1:T(8,128)S(1)}, f32[1024,128]{0,1:T(8,128)S(1)}, bf16[512,640]{1,0:T(8,128)(2,1)S(1)}) conditional(s32[]{:T(128)} %clamp.2, (pred[1024,1024]{0,1:T(8,128)(4,1)}, bf16[1024,128]{1,0:T(8,128)(2,1)S(1)}, bf16[512,5,128]{0,2,1:T(8,128)(2,1)S(1)}, f32[5,512]{1,0:T(8,128)}, ...), branch_computations={%region_42.43_spmd, %region_43.44_spmd, %region_44.45_spmd, %regio... | conditional | flops 3385587200 | bytes 72020072 | solution.py:171
  359.3 3.4 fusion.185
  362.7 3.3 fusion.178
  377.3 4.7 %fusion.322 = bf16[5,512,512]{1,2,0:T(8,128)(2,1)S(1)} fusion(f32[512,512,5]{1,0,2:T(8,128)} %copy-done.9, f32[5,512]{1,0:T(8,128)} %get-tuple-element.741, f32[5,512]{1,0:T(8,128)S(1)} %copy-done.60, pred[512,512]{0,1:T(8,128)(4,1)} %copy-done.26, bf16[512,5,128]{0,2,1:T(8,128)(2,1)} %bitcast.901, bf16[1024,256]{1,0:T(8,128)(2,1)} %param.30), kind=kOutput, calls=%fused_computation.384 | convolution fusion | flops 344719360 | bytes 8939520 | tf_op jit(solution)/shard_map/rgd,kd->grk/dot_general | solution.py:45
  387.2 4.6 %fusion.325 = bf16[5,512,512]{1,2,0:T(8,128)(2,1)S(1)} fusion(f32[512,512,5]{1,0,2:T(8,128)} %copy-done.8, f32[5,512]{1,0:T(8,128)S(1)} %copy-done.62, f32[5,512]{1,0:T(8,128)S(1)} %copy-done.59, pred[512,512]{0,1:T(8,128)(4,1)S(1)} %copy-done.27, bf16[512,5,128]{0,2,1:T(8,128)(2,1)S(1)} %bitcast.898, bf16[1024,256]{1,0:T(8,128)(2,1)} %param.30), kind=kOutput, calls=%fused_computation.388 | convolution fusion | flops 344719360 | bytes 8933376 | tf_op jit(solution)/shard_map/rgd,kd->grk/dot_general | solution.py:45
  394.4 3.3 convolution_convert_fusion.12
  399.9 4.1 convolution_bitcast_fusion.10
  411.4 3.2 maximum_maximum_fusion
  414.6 6.1 %copy.644 = bf16[1280,2560]{1,0:T(8,128)(2,1)} copy(bf16[1280,2560]{1,0:T(8,128)(2,1)} %all-gather.9.cloned.1.call-done) | data formatting | bytes 13107200
  (178 shorter events, 111.9 us)
Async XLA Ops:
  7.2 89.8 %all-gather.5.cloned.1.call-start = ((), (), s32[]{:S(2)}) async-start(), calls=%async_computation.1 | async-start | bytes 6553600 | tf_op jit(solution)/shard_map/all_gather | solution.py:219
  7.9 112.3 %all-gather.7.cloned.1.call-start = ((), (), s32[]{:S(2)}) async-start(), calls=%async_computation.2 | async-start | bytes 6758400 | tf_op jit(solution)/shard_map/all_gather | solution.py:223
  8.6 269.0 %reduce-scatter.2.cloned.1.call-start = ((), (), s32[]{:S(2)}) async-start(), calls=%async_computation.3 | async-start | bytes 13516800 | tf_op jit(solution)/shard_map/reduce_scatter | solution.py:230
  34.2 35.5 %copy-start.2 = (pred[1024,1024]{0,1:T(8,128)(4,1)}, pred[1024,1024]{0,1:T(8,128)(4,1)S(1)}, u32[]{:S(2)}) copy-start(pred[1024,1024]{0,1:T(8,128)(4,1)S(1)} %fusion.328) | copy-start | bytes 3145732
  34.2 116.6 %copy-start.26 = (pred[512,512]{0,1:T(8,128)(4,1)}, pred[512,512]{0,1:T(8,128)(4,1)S(1)}, u32[]{:S(2)}) copy-start(pred[512,512]{0,1:T(8,128)(4,1)S(1)} %slice.324) | copy-start | bytes 786436
  39.0 30.7 %copy-start = (bf16[512,640]{0,1:T(8,128)(2,1)}, bf16[512,640]{0,1:T(8,128)(2,1)S(1)}, u32[]{:S(2)}) copy-start(bf16[512,640]{0,1:T(8,128)(2,1)S(1)} %copy.579) | copy-start | bytes 1966084
  45.7 23.9 %copy-start.3 = (bf16[1024,128]{1,0:T(8,128)(2,1)}, bf16[1024,128]{1,0:T(8,128)(2,1)S(1)}, u32[]{:S(2)}) copy-start(bf16[1024,128]{1,0:T(8,128)(2,1)S(1)} %get-tuple-element.746) | copy-start | bytes 786436
  69.6 77.5 %copy-start.5 = (bf16[512,5,128]{2,0,1:T(8,128)(2,1)}, bf16[512,5,128]{2,0,1:T(8,128)(2,1)S(1)}, u32[]{:S(2)}) copy-start(bf16[512,5,128]{2,0,1:T(8,128)(2,1)S(1)} %get-tuple-element.364) | copy-start | bytes 1966084
  69.6 17.1 %copy-start.57 = (s32[1024]{0:T(1024)S(1)}, s32[1024]{0:T(1024)}, u32[]{:S(2)}) copy-start(s32[1024]{0:T(1024)} %param.35) | copy-start | bytes 12292
  85.4 7.5 %copy-start.6 = (bf16[512,5,128]{2,0,1:T(8,128)(2,1)}, bf16[512,5,128]{2,0,1:T(8,128)(2,1)S(1)}, u32[]{:S(2)}) copy-start(bf16[512,5,128]{2,0,1:T(8,128)(2,1)S(1)} %get-tuple-element.363) | copy-start | bytes 1966084
  97.0 53.8 %copy-start.58 = (f32[5,512]{1,0:T(8,128)}, f32[5,512]{1,0:T(8,128)S(1)}, u32[]{:S(2)}) copy-start(f32[5,512]{1,0:T(8,128)S(1)} %get-tuple-element.748) | copy-start | bytes 30724
  148.3 7.8 %copy-start.7 = (bf16[512,5,128]{2,0,1:T(8,128)(2,1)S(1)}, bf16[512,5,128]{2,0,1:T(8,128)(2,1)}, u32[]{:S(2)}) copy-start(bf16[512,5,128]{2,0,1:T(8,128)(2,1)} %copy-done.6) | copy-start | bytes 1966084
  172.5 242.1 %all-gather.9.cloned.1.call-start = ((), (), s32[]{:S(2)}) async-start(), calls=%async_computation.4 | async-start | bytes 6758400 | tf_op jit(solution)/shard_map/all_gather | solution.py:231
  279.3 51.7 %copy-start.1 = (bf16[512,640]{0,1:T(8,128)(2,1)S(1)}, bf16[512,640]{0,1:T(8,128)(2,1)}, u32[]{:S(2)}) copy-start(bf16[512,640]{0,1:T(8,128)(2,1)} %copy-done) | copy-start | bytes 1966084
  279.3 51.7 %copy-start.4 = (bf16[1024,128]{1,0:T(8,128)(2,1)S(1)}, bf16[1024,128]{1,0:T(8,128)(2,1)}, u32[]{:S(2)}) copy-start(bf16[1024,128]{1,0:T(8,128)(2,1)} %copy-done.3) | copy-start | bytes 786436
  331.1 46.3 %copy-start.60 = (f32[5,512]{1,0:T(8,128)S(1)}, f32[5,512]{1,0:T(8,128)}, u32[]{:S(2)}) copy-start(f32[5,512]{1,0:T(8,128)} %get-tuple-element.747) | copy-start | bytes 30724
  376.4 5.6 %copy-start.11 = (bf16[512,640]{1,0:T(8,128)(2,1)}, bf16[512,640]{1,0:T(8,128)(2,1)S(1)}, u32[]{:S(2)}) copy-start(bf16[512,640]{1,0:T(8,128)(2,1)S(1)} %get-tuple-element.702) | copy-start | bytes 1966084
  382.0 5.1 %copy-start.14 = (bf16[512,640]{0,1:T(8,128)(2,1)S(1)}, bf16[512,640]{0,1:T(8,128)(2,1)}, u32[]{:S(2)}) copy-start(bf16[512,640]{0,1:T(8,128)(2,1)} %copy.283) | copy-start | bytes 1966084
  382.0 5.1 %copy-start.27 = (pred[512,512]{0,1:T(8,128)(4,1)S(1)}, pred[512,512]{0,1:T(8,128)(4,1)}, u32[]{:S(2)}) copy-start(pred[512,512]{0,1:T(8,128)(4,1)} %copy-done.26) | copy-start | bytes 786436
  382.1 5.1 %copy-start.59 = (f32[5,512]{1,0:T(8,128)S(1)}, f32[5,512]{1,0:T(8,128)}, u32[]{:S(2)}) copy-start(f32[5,512]{1,0:T(8,128)} %copy-done.58) | copy-start | bytes 30724
  382.1 5.1 %copy-start.62 = (f32[5,512]{1,0:T(8,128)S(1)}, f32[5,512]{1,0:T(8,128)}, u32[]{:S(2)}) copy-start(f32[5,512]{1,0:T(8,128)} %get-tuple-element.743) | copy-start | bytes 30724
  387.2 6.1 %copy-start.30 = (f32[1024,128]{0,1:T(8,128)S(1)}, f32[1024,128]{0,1:T(8,128)}, u32[]{:S(2)}) copy-start(f32[1024,128]{0,1:T(8,128)} %copy-done.29) | copy-start | bytes 1572868
  391.8 8.1 %copy-start.15 = (bf16[512,640]{0,1:T(8,128)(2,1)S(1)}, bf16[512,640]{0,1:T(8,128)(2,1)}, u32[]{:S(2)}) copy-start(bf16[512,640]{0,1:T(8,128)(2,1)} %copy.306) | copy-start | bytes 1966084
  394.4 9.8 %slice-start = ((s8[5242880]{0:T(1024)(128)(4,1)}), s8[1048576]{0:T(1024)(128)(4,1)S(1)}, s32[]{:S(2)}) async-start(s8[5242880]{0:T(1024)(128)(4,1)} %bitcast.889), calls=%async_computation.5 | async-start | bytes 2097152
  (20 other events, 49.8 us)
Sparse Core Ops, SparseCore 0:
  9.7 59.4 all-gather.4
  71.4 48.6 all-gather.6
  172.6 104.9 reduce-scatter.1
  279.7 48.0 all-gather.8

commit v2 on v0

--- a/solution.py
+++ b/solution.py
@@ -4,6 +4,7 @@
 import jax.numpy as jnp
 from jax import lax
 from jax.sharding import PartitionSpec as P
+
 
 QUERY_HEADS = 40
 KEY_VALUE_HEADS = 8
@@ -117,87 +118,91 @@
     return (jnp.concatenate(outs, axis=1), jnp.stack(logs, axis=0))
 
 
+def cluster_backward(
+    head_cluster, query, keys, values, layout, attn_rows, log_rows, grad_rows, factor
+):
+    allowed, half_rows, key_step, bucket = layout
+    row_count = query.shape[0]
+    group_size = QUERY_HEADS // KEY_VALUE_HEADS
+    span = slice(
+        head_cluster * group_size * HEAD_SIZE, (head_cluster + 1) * group_size * HEAD_SIZE
+    )
+    query_part = query[:, span].reshape(row_count, group_size, HEAD_SIZE)
+    attn_part = attn_rows[:, span].reshape(row_count, group_size, HEAD_SIZE)
+    grad_part = grad_rows[:, span].reshape(row_count, group_size, HEAD_SIZE)
+    key_part = keys[:, head_cluster * HEAD_SIZE : (head_cluster + 1) * HEAD_SIZE]
+    value_part = values[:, head_cluster * HEAD_SIZE : (head_cluster + 1) * HEAD_SIZE]
+    log_part = log_rows[head_cluster]
+    early_query, early_key, early_value = block_backward(
+        query_part[:half_rows],
+        key_part[:half_rows],
+        value_part[:half_rows],
+        allowed[:half_rows, :half_rows],
+        attn_part[:half_rows],
+        log_part[:, :half_rows],
+        grad_part[:half_rows],
+        factor,
+    )
+
+    def later_block(bucket_id):
+        first_key = bucket_id * key_step
+
+        def run_block(operands):
+            query_late, key_all, value_all, attn_late, log_late, grad_late = operands
+            late_query, late_key, late_value = block_backward(
+                query_late,
+                key_all[first_key:],
+                value_all[first_key:],
+                allowed[half_rows:, first_key:],
+                attn_late,
+                log_late,
+                grad_late,
+                factor,
+            )
+            return (
+                late_query,
+                jnp.pad(late_key, ((first_key, 0), (0, 0))),
+                jnp.pad(late_value, ((first_key, 0), (0, 0))),
+            )
+
+        return run_block
+
+    late_query, late_key, late_value = lax.switch(
+        bucket,
+        [later_block(bucket_id) for bucket_id in range(5)],
+        (
+            query_part[half_rows:],
+            key_part,
+            value_part,
+            attn_part[half_rows:],
+            log_part[:, half_rows:],
+            grad_part[half_rows:],
+        ),
+    )
+    tail_rows = row_count - half_rows
+    key_total = late_key + jnp.pad(early_key, ((0, tail_rows), (0, 0)))
+    value_total = late_value + jnp.pad(early_value, ((0, tail_rows), (0, 0)))
+    query_out = (
+        jnp.concatenate([early_query, late_query], axis=0)
+        .astype(jnp.bfloat16)
+        .reshape(row_count, group_size * HEAD_SIZE)
+    )
+    return (query_out, key_total.astype(jnp.bfloat16), value_total.astype(jnp.bfloat16))
+
+
 def pack_backward(query, keys, values, doc_ids, attn_rows, log_rows, grad_rows, factor):
-    allowed, half_rows, key_step, bucket = pack_layout(doc_ids)
-    row_count = doc_ids.shape[0]
-    group_size = QUERY_HEADS // KEY_VALUE_HEADS
-    query_parts = []
-    key_parts = []
-    value_parts = []
+    layout = pack_layout(doc_ids)
+    parts = []
     for head_cluster in range(keys.shape[1] // HEAD_SIZE):
-        span = slice(
-            head_cluster * group_size * HEAD_SIZE, (head_cluster + 1) * group_size * HEAD_SIZE
-        )
-        query_part = query[:, span].reshape(row_count, group_size, HEAD_SIZE)
-        attn_part = attn_rows[:, span].reshape(row_count, group_size, HEAD_SIZE)
-        grad_part = grad_rows[:, span].reshape(row_count, group_size, HEAD_SIZE)
-        key_part = keys[:, head_cluster * HEAD_SIZE : (head_cluster + 1) * HEAD_SIZE]
-        value_part = values[:, head_cluster * HEAD_SIZE : (head_cluster + 1) * HEAD_SIZE]
-        log_part = log_rows[head_cluster]
-        early_query, early_key, early_value = block_backward(
-            query_part[:half_rows],
-            key_part[:half_rows],
-            value_part[:half_rows],
-            allowed[:half_rows, :half_rows],
-            attn_part[:half_rows],
-            log_part[:, :half_rows],
-            grad_part[:half_rows],
-            factor,
-        )
-
-        def later_block(bucket_id):
-            first_key = bucket_id * key_step
-
-            def run_block(operands):
-                query_late, key_all, value_all, attn_late, log_late, grad_late = operands
-                late_query, late_key, late_value = block_backward(
-                    query_late,
-                    key_all[first_key:],
-                    value_all[first_key:],
-                    allowed[half_rows:, first_key:],
-                    attn_late,
-                    log_late,
-                    grad_late,
-                    factor,
-                )
-                return (
-                    late_query,
-                    jnp.pad(late_key, ((first_key, 0), (0, 0))),
-                    jnp.pad(late_value, ((first_key, 0), (0, 0))),
-                )
-
-            return run_block
-
-        late_query, late_key, late_value = lax.switch(
-            bucket,
-            [later_block(bucket_id) for bucket_id in range(5)],
-            (
-                query_part[half_rows:],
-                key_part,
-                value_part,
-                attn_part[half_rows:],
-                log_part[:, half_rows:],
-                grad_part[half_rows:],
-            ),
-        )
-        tail_rows = row_count - half_rows
-        key_total = late_key + jnp.pad(early_key, ((0, tail_rows), (0, 0)))
-        value_total = late_value + jnp.pad(early_value, ((0, tail_rows), (0, 0)))
-        query_parts.append(
-            jnp.concatenate([early_query, late_query], axis=0)
-            .astype(jnp.bfloat16)
-            .reshape(row_count, group_size * HEAD_SIZE)
-        )
-        key_parts.append(key_total.astype(jnp.bfloat16))
-        value_parts.append(value_total.astype(jnp.bfloat16))
-    return (
-        jnp.concatenate(query_parts, axis=1),
-        jnp.concatenate(key_parts, axis=1),
-        jnp.concatenate(value_parts, axis=1),
-    )
-
-
-def shards(query, keys, values, out_weight, loss_grad, lengths, languages, labels):
+        parts.append(
+            cluster_backward(
+                head_cluster, query, keys, values, layout, attn_rows, log_rows, grad_rows, factor
+            )
+        )
+    return tuple(jnp.concatenate([part[k] for part in parts], axis=1) for k in range(3))
+
+
+def layer(query, keys, values, out_weight, loss_grad, lengths, languages, labels):
     factor = 1.0 / math.sqrt(HEAD_SIZE)
     row_count = query.shape[0]
     doc_ids = token_docs(lengths[0], row_count)
@@ -211,7 +216,10 @@
     counted = labels != -100
     lang_match = token_lang[:, None] == jnp.arange(LANGS, dtype=jnp.int32)[None, :]
     local_counts = jnp.sum((lang_match & counted[:, None]).astype(jnp.int32), axis=0)
-    counts = lax.psum(local_counts, "dp").astype(jnp.float32)
+    padded_counts = jnp.pad(local_counts, (0, 128 - LANGS))[None, :]
+    counts = jnp.sum(lax.all_gather(padded_counts, "dp", axis=0, tiled=True), axis=0)[:LANGS].astype(
+        jnp.float32
+    )
     lang_weight = jnp.sqrt(jnp.sum(counts) / (LANGS * jnp.maximum(counts, 1.0)))
     token_weight = jnp.where(
         counted, jnp.sum(jnp.where(lang_match, lang_weight[None, :], 0.0), axis=1), 0.0
@@ -227,7 +235,10 @@
     local_term = lax.dot_general(
         attention_result, weighted, (((0,), (0,)), ((), ())), preferred_element_type=jnp.float32
     )
-    projection_gradient = lax.psum(local_term, "dp").astype(jnp.bfloat16)
+    projection_part = lax.psum_scatter(
+        local_term.astype(jnp.bfloat16), "dp", scatter_dimension=0, tiled=True
+    )
+    projection_gradient = lax.all_gather(projection_part, "dp", axis=0, tiled=True)
     query_gradient, key_gradient, value_gradient = pack_backward(
         query, keys, values, doc_ids, attention_result, log_rows, out_grad, factor
     )
@@ -252,4 +263,4 @@
         P("dp", "tensor"),
         P("tensor", None),
     )
-    return jax.shard_map(shards, mesh=mesh, in_specs=in_specs, out_specs=out_specs, check_vma=False)
+    return jax.shard_map(layer, mesh=mesh, in_specs=in_specs, out_specs=out_specs, check_vma=False)

time: 496 us -> 416 us (0.84)
  the two profiles are of different devices: /device:TPU:0 before, /device:TPU:6 now
where the time goes in v2:
time: 416 us; the launch traced here: 408 us
  waiting for transfers between devices  112 us (27%)
  matrix products  107 us (26%)
  local copies, waits for them, and re-layouts  70.3 us (17%)
  loops' own time  55.5 us (13%)
  other arithmetic  24.9 us (6%)
  blocking collectives  20.9 us (5%)
  between operations  17 us (4%)
    reduce_scatter x1, waiting for transfers between devices, layer(): lax.psum_scatter(local_term.astype(jnp.bfloat16), 'dp', scatter_dimension...  86.1 us
    another operation x2, loops' own time, cluster_backward(): lax.switch(bucket, [later_block(bucket_id) for bucket_id in range(5)], (q...  38.5 us
    unnamed x63, local copies, waits for them, and re-layouts  25.9 us
    all_gather x1, waiting for transfers between devices, layer(): lax.all_gather(out_weight, 'dp', axis=1, tiled=True)  25 us
    all_gather x1, blocking collectives, layer(): lax.all_gather(padded_counts, 'dp', axis=0, tiled=True)  20.9 us
    dot_general x4, matrix products, block_forward(): jnp.einsum('grk,kd->rgd', weights, value_rows, preferred_element_type=jnp...  18.4 us
    dot_general x4, matrix products, block_backward(): jnp.einsum('rgd,kd->grk', grad_rows, value_rows, preferred_element_type=j...  18.2 us
    unnamed x2, loops' own time  16.9 us
  transfers between devices with their start and end apart: 4, of which 2 were waited for; matrix products, arithmetic and copies ran while one was open for 34% of the time, Pallas kernels for 0%

profile of v2, /device:TPU:6, one launch (start us, length us, event | category | flops | bytes accessed | tf_op | source)
XLA Modules:
  0.0 407.9 jit_solution(13292419729147206652)
XLA Ops:
  15.6 20.9 %all-gather.1 = s32[32,1,128]{2,1,0:T(1,128)S(1)} all-gather(s32[1,1,128]{2,1,0:T(1,128)S(1)} %pad_bitcast_fusion), channel_id=2, replica_groups=mesh['dp'=32,'tensor'=4] {'dp'}, dimensions={0}, use_global_device_ids=true | all-gather | bytes 16896 | tf_op jit(solution)/shard_map/all_gather | solution.py:220
  37.2 3.4 fusion.355
  48.6 21.9 %conditional.9 = (f32[5,512]{1,0:T(8,128)}, bf16[512,5,128]{2,0,1:T(8,128)(2,1)S(1)}) conditional(s32[]{:T(128)} %clamp.2, (pred[1024,1024]{0,1:T(8,128)(4,1)S(1)}, bf16[1024,128]{1,0:T(8,128)(2,1)}, bf16[512,5,128]{0,2,1:T(8,128)(2,1)}, bf16[1024,128]{1,0:T(8,128)(2,1)}) %tuple.143, ...), branch_computations={%region_22.25_spmd, %region_25.28_spmd, %region_28.31_spmd, %regio... | conditional | flops 1371338240 | bytes 35985424
  54.6 3.9 fusion.72
  71.3 12.3 %conditional.8 = (f32[5,512]{1,0:T(8,128)}, bf16[512,5,128]{2,0,1:T(8,128)(2,1)S(1)}) conditional(s32[]{:T(128)} %clamp.2, (pred[1024,1024]{0,1:T(8,128)(4,1)S(1)}, bf16[1024,128]{1,0:T(8,128)(2,1)S(1)}, bf16[512,5,128]{0,2,1:T(8,128)(2,1)S(1)}, bf16[1024,128]{1,0:T(8,128)(2,1)}) %tuple.315, ...), branch_computations={%region_5.8_spmd, %region_8.11_spmd, %region_11.14_spmd, %region_1... | conditional | flops 1371338240 | bytes 37034028
  75.5 3.6 fusion.14
  95.2 25.0 %all-gather.8.cloned.1.call-done = bf16[1280,2560]{0,1:T(8,128)(2,1)} async-done(((bf16[1280,80]{0,1:T(8,128)(2,1)}), bf16[1280,2560]{0,1:T(8,128)(2,1)}) %all-gather.8.cloned.1.call-update) | async-done | bytes 6553616 | tf_op jit(solution)/shard_map/all_gather | solution.py:231
  120.1 11.4 %convolution_convert_fusion.11 = bf16[1024,1280]{1,0:T(8,128)(2,1)S(1)} fusion(bf16[1280,2560]{0,1:T(8,128)(2,1)} %all-gather.8.cloned.1.call-done, bf16[1024,2560]{1,0:T(8,128)(2,1)} %all-gather.6.cloned.1.call-done, f32[1024]{0:T(1024)} %broadcast_select_fusion), kind=kOutput, calls=%fused_computation.400 | convolution fusion | flops 6720061440 | bytes 14422016 | tf_op jit(solution)/shard_map/dot_general | solution.py:229
  141.8 5.4 %multiply_reduce_fusion.10 = (f32[5,512]{1,0:T(8,128)}, bf16[5,512,128]{2,1,0:T(8,128)(2,1)S(1)}) fusion(f32[5,512,128]{2,1,0:T(8,128)} %copy.629, bf16[1024,256]{1,0:T(8,128)(2,1)} %param.30, f32[512,512,5]{1,0,2:T(8,128)} %copy-done.6, f32[5,512]{1,0:T(8,128)} %get-tuple-element.862, pred[512,512]{0,1:T(8,128)(4,1)} %copy-done.24), kind=kOutput, calls=%fused_computation.411 | convolution fusion | flops 342095360 | bytes 7628800 | tf_op jit(solution)/shard_map/grk,kd->rgd/dot_general | solution.py:34
  150.8 5.4 %multiply_reduce_fusion.11 = (f32[5,512]{1,0:T(8,128)}, bf16[5,512,128]{2,1,0:T(8,128)(2,1)S(1)}) fusion(f32[5,512,128]{2,1,0:T(8,128)} %copy.619, bf16[1024,256]{1,0:T(8,128)(2,1)} %param.30, f32[512,512,5]{1,0,2:T(8,128)} %copy-done.5, f32[5,512]{1,0:T(8,128)S(1)} %get-tuple-element.863, pred[512,512]{0,1:T(8,128)(4,1)} %copy-done.24), kind=kOutput, calls=%fused_computation.412 | convolution fusion | flops 342095360 | bytes 7622656 | tf_op jit(solution)/shard_map/grk,kd->rgd/dot_general | solution.py:34
  159.9 11.6 %convolution_convert_fusion.10 = bf16[1280,2560]{1,0:T(8,128)(2,1)} fusion(bf16[1024,2560]{1,0:T(8,128)(2,1)} %all-gather.6.cloned.1.call-done, f32[1024]{0:T(1024)S(1)} %copy-done.57, bf16[1024,640]{0,1:T(8,128)(2,1)} %bitcast.886, bf16[1024,640]{0,1:T(8,128)(2,1)} %bitcast.888), kind=kOutput, calls=%fused_computation.380 | convolution fusion | flops 6727270400 | bytes 14422016 | tf_op jit(solution)/shard_map/dot_general | solution.py:235
  171.6 86.1 %reduce-scatter.2.cloned.1.call-done = bf16[40,2560]{1,0:T(8,128)(2,1)} async-done(((bf16[1280,2560]{1,0:T(8,128)(2,1)}), bf16[40,2560]{1,0:T(8,128)(2,1)}) %reduce-scatter.2.cloned.1.call-update) | async-done | bytes 204816 | tf_op jit(solution)/shard_map/reduce_scatter | solution.py:238
  257.7 55.1 %conditional.11 = (f32[1024,128]{0,1:T(8,128)}, f32[1024,128]{0,1:T(8,128)}, bf16[512,640]{1,0:T(8,128)(2,1)}) conditional(s32[]{:T(128)} %clamp.2, (pred[1024,1024]{0,1:T(8,128)(4,1)}, bf16[1024,128]{1,0:T(8,128)(2,1)}, bf16[512,5,128]{0,2,1:T(8,128)(2,1)}, f32[5,512]{1,0:T(8,128)}, bf16[1024,128]{1,0:T(8,128)(2,1)}, ...), branch_computations={%region_47.48_spmd, %region_48.49_spmd, %region_49.50_spmd, %regio... | conditional | flops 3385587200 | bytes 70971472 | solution.py:170
  279.9 4.2 %fusion.245 = f32[896,128]{0,1:T(8,128)} fusion(bf16[512,5,128]{0,2,1:T(8,128)(2,1)S(1)} %bitcast.906, f32[896,512,5]{1,0,2:T(8,128)S(1)} %fusion.250, f32[5,512]{1,0:T(8,128)} %get-tuple-element.323, pred[512,896]{0,1:T(8,128)(4,1)S(1)} %copy-done.35), kind=kOutput, calls=%fused_computation.300 | convolution fusion | flops 596377600 | bytes 10758144 | tf_op jit(solution)/shard_map/cond/branch_1_fun/grk,rgd->kd/dot_general | solution.py:43
  284.0 4.5 %fusion.238 = bf16[5,512,896]{1,2,0:T(8,128)(2,1)S(1)} fusion(f32[896,512,5]{1,0,2:T(8,128)S(1)} %fusion.250, f32[5,512]{1,0:T(8,128)S(1)} %copy.568, f32[5,512]{1,0:T(8,128)} %get-tuple-element.323, pred[512,896]{0,1:T(8,128)(4,1)S(1)} %copy-done.35, bf16[512,5,128]{0,2,1:T(8,128)(2,1)S(1)} %bitcast.907, bf16[1024,128]{1,0:T(8,128)(2,1)} %get-tuple-element.324), kind=kOutput, calls=%fused_computation.291 | convolution fusion | flops 603258880 | bytes 15132672 | tf_op jit(solution)/shard_map/cond/branch_1_fun/rgd,kd->grk/dot_general | solution.py:46
  288.5 3.4 convolution_bitcast_fusion.6
  312.9 41.7 %conditional.10 = (f32[1024,128]{0,1:T(8,128)S(1)}, f32[1024,128]{0,1:T(8,128)S(1)}, bf16[512,640]{1,0:T(8,128)(2,1)S(1)}) conditional(s32[]{:T(128)} %clamp.2, (pred[1024,1024]{0,1:T(8,128)(4,1)}, bf16[1024,128]{1,0:T(8,128)(2,1)S(1)}, bf16[512,5,128]{0,2,1:T(8,128)(2,1)S(1)}, f32[5,512]{1,0:T(8,128)}, ...), branch_computations={%region_42.43_spmd, %region_43.44_spmd, %region_44.45_spmd, %regio... | conditional | flops 3385587200 | bytes 72020072 | solution.py:170
  330.5 3.4 fusion.143
  333.9 4.4 %fusion.136 = bf16[5,512,896]{1,2,0:T(8,128)(2,1)S(1)} fusion(f32[896,512,5]{1,0,2:T(8,128)S(1)} %fusion.148, f32[5,512]{1,0:T(8,128)S(1)} %copy.508, f32[5,512]{1,0:T(8,128)} %get-tuple-element.288, pred[512,896]{0,1:T(8,128)(4,1)S(1)} %copy-done.36, bf16[512,5,128]{0,2,1:T(8,128)(2,1)S(1)} %bitcast.922, bf16[1024,128]{1,0:T(8,128)(2,1)S(1)} %copy-done.50), kind=kOutput, calls=%fused_computation.179 | convolution fusion | flops 603258880 | bytes 15132672 | tf_op jit(solution)/shard_map/cond/branch_1_fun/rgd,kd->grk/dot_general | solution.py:46
  355.5 4.7 %fusion.322 = bf16[5,512,512]{1,2,0:T(8,128)(2,1)S(1)} fusion(f32[512,512,5]{1,0,2:T(8,128)} %copy-done.6, f32[5,512]{1,0:T(8,128)} %get-tuple-element.856, f32[5,512]{1,0:T(8,128)} %get-tuple-element.862, pred[512,512]{0,1:T(8,128)(4,1)} %copy-done.24, bf16[512,5,128]{0,2,1:T(8,128)(2,1)} %bitcast.900, bf16[1024,256]{1,0:T(8,128)(2,1)} %param.30), kind=kOutput, calls=%fused_computation.385 | convolution fusion | flops 344719360 | bytes 8945664 | tf_op jit(solution)/shard_map/rgd,kd->grk/dot_general | solution.py:46
  367.2 4.8 %fusion.325 = bf16[5,512,512]{1,2,0:T(8,128)(2,1)S(1)} fusion(f32[512,512,5]{1,0,2:T(8,128)} %copy-done.5, f32[5,512]{1,0:T(8,128)} %get-tuple-element.858, f32[5,512]{1,0:T(8,128)S(1)} %copy-done.56, pred[512,512]{0,1:T(8,128)(4,1)S(1)} %copy-done.25, bf16[512,5,128]{0,2,1:T(8,128)(2,1)} %bitcast.897, bf16[1024,256]{1,0:T(8,128)(2,1)} %param.30), kind=kOutput, calls=%fused_computation.389 | convolution fusion | flops 344719360 | bytes 8939520 | tf_op jit(solution)/shard_map/rgd,kd->grk/dot_general | solution.py:46
  378.0 4.1 convolution_bitcast_fusion.10
  382.2 4.0 convolution_bitcast_fusion.11
  395.1 6.1 %copy.771 = bf16[1280,2560]{1,0:T(8,128)(2,1)} copy(bf16[1280,2560]{1,0:T(8,128)(2,1)} %all-gather.10.cloned.1.call-done) | data formatting | bytes 13107200
  (157 shorter events, 115.2 us)
Async XLA Ops:
  7.2 88.0 %all-gather.6.cloned.1.call-start = ((), (), s32[]{:S(2)}) async-start(), calls=%async_computation.1 | async-start | bytes 6553600 | tf_op jit(solution)/shard_map/all_gather | solution.py:227
  7.9 112.2 %all-gather.8.cloned.1.call-start = ((), (), s32[]{:S(2)}) async-start(), calls=%async_computation.2 | async-start | bytes 6758400 | tf_op jit(solution)/shard_map/all_gather | solution.py:231
  8.6 249.0 %reduce-scatter.2.cloned.1.call-start = ((), (), s32[]{:S(2)}) async-start(), calls=%async_computation.3 | async-start | bytes 6758400 | tf_op jit(solution)/shard_map/reduce_scatter | solution.py:238
  37.2 33.3 %copy-start = (pred[1024,1024]{0,1:T(8,128)(4,1)}, pred[1024,1024]{0,1:T(8,128)(4,1)S(1)}, u32[]{:S(2)}) copy-start(pred[1024,1024]{0,1:T(8,128)(4,1)S(1)} %fusion.328) | copy-start | bytes 3145732
  37.2 53.9 %copy-start.24 = (pred[512,512]{0,1:T(8,128)(4,1)}, pred[512,512]{0,1:T(8,128)(4,1)S(1)}, u32[]{:S(2)}) copy-start(pred[512,512]{0,1:T(8,128)(4,1)S(1)} %slice.328) | copy-start | bytes 786436
  70.5 14.5 %copy-start.54 = (s32[1024]{0:T(1024)S(1)}, s32[1024]{0:T(1024)}, u32[]{:S(2)}) copy-start(s32[1024]{0:T(1024)} %param.35) | copy-start | bytes 12292
  83.6 7.5 %copy-start.3 = (bf16[512,5,128]{2,0,1:T(8,128)(2,1)}, bf16[512,5,128]{2,0,1:T(8,128)(2,1)S(1)}, u32[]{:S(2)}) copy-start(bf16[512,5,128]{2,0,1:T(8,128)(2,1)S(1)} %get-tuple-element.363) | copy-start | bytes 1966084
  83.6 4.2 %copy-start.29 = (bf16[512,640]{0,1:T(8,128)(2,1)S(1)}, bf16[512,640]{0,1:T(8,128)(2,1)}, u32[]{:S(2)}) copy-start(bf16[512,640]{0,1:T(8,128)(2,1)} %copy.708) | copy-start | bytes 1966084
  95.2 55.7 %copy-start.55 = (f32[5,512]{1,0:T(8,128)}, f32[5,512]{1,0:T(8,128)S(1)}, u32[]{:S(2)}) copy-start(f32[5,512]{1,0:T(8,128)S(1)} %get-tuple-element.863) | copy-start | bytes 30724
  141.8 5.5 %copy-start.2 = (bf16[512,5,128]{2,0,1:T(8,128)(2,1)S(1)}, bf16[512,5,128]{2,0,1:T(8,128)(2,1)}, u32[]{:S(2)}) copy-start(bf16[512,5,128]{2,0,1:T(8,128)(2,1)} %copy-done.1) | copy-start | bytes 1966084
  150.8 5.4 %copy-start.4 = (bf16[512,5,128]{2,0,1:T(8,128)(2,1)S(1)}, bf16[512,5,128]{2,0,1:T(8,128)(2,1)}, u32[]{:S(2)}) copy-start(bf16[512,5,128]{2,0,1:T(8,128)(2,1)} %copy-done.3) | copy-start | bytes 1966084
  156.2 3.7 copy-start.57
  171.5 223.6 %all-gather.10.cloned.1.call-start = ((), (), s32[]{:S(2)}) async-start(), calls=%async_computation.4 | async-start | bytes 6758400 | tf_op jit(solution)/shard_map/all_gather | solution.py:241
  330.5 3.5 copy-start.50
  354.6 5.6 %copy-start.8 = (bf16[512,640]{1,0:T(8,128)(2,1)}, bf16[512,640]{1,0:T(8,128)(2,1)S(1)}, u32[]{:S(2)}) copy-start(bf16[512,640]{1,0:T(8,128)(2,1)S(1)} %get-tuple-element.817) | copy-start | bytes 1966084
  360.2 6.9 %copy-start.25 = (pred[512,512]{0,1:T(8,128)(4,1)S(1)}, pred[512,512]{0,1:T(8,128)(4,1)}, u32[]{:S(2)}) copy-start(pred[512,512]{0,1:T(8,128)(4,1)} %copy-done.24) | copy-start | bytes 786436
  360.2 6.9 %copy-start.56 = (f32[5,512]{1,0:T(8,128)S(1)}, f32[5,512]{1,0:T(8,128)}, u32[]{:S(2)}) copy-start(f32[5,512]{1,0:T(8,128)} %copy-done.55) | copy-start | bytes 30724
  362.8 4.3 %copy-start.26 = (f32[1024,128]{0,1:T(8,128)S(1)}, f32[1024,128]{0,1:T(8,128)}, u32[]{:S(2)}) copy-start(f32[1024,128]{0,1:T(8,128)} %get-tuple-element.818) | copy-start | bytes 1572868
  367.2 4.8 %copy-start.7 = (bf16[512,640]{0,1:T(8,128)(2,1)S(1)}, bf16[512,640]{0,1:T(8,128)(2,1)}, u32[]{:S(2)}) copy-start(bf16[512,640]{0,1:T(8,128)(2,1)} %copy.706) | copy-start | bytes 1966084
  367.2 6.3 %copy-start.28 = (f32[1024,128]{0,1:T(8,128)S(1)}, f32[1024,128]{0,1:T(8,128)}, u32[]{:S(2)}) copy-start(f32[1024,128]{0,1:T(8,128)} %copy-done.27) | copy-start | bytes 1572868
  372.0 6.0 %copy-start.12 = (bf16[512,640]{0,1:T(8,128)(2,1)S(1)}, bf16[512,640]{0,1:T(8,128)(2,1)}, u32[]{:S(2)}) copy-start(bf16[512,640]{0,1:T(8,128)(2,1)} %copy.434) | copy-start | bytes 1966084
  376.9 5.2 %copy-start.30 = (f32[1024,128]{0,1:T(8,128)S(1)}, f32[1024,128]{0,1:T(8,128)}, u32[]{:S(2)}) copy-start(f32[1024,128]{0,1:T(8,128)} %get-tuple-element.819) | copy-start | bytes 1572868
  378.0 4.2 %copy-start.11 = (bf16[512,640]{0,1:T(8,128)(2,1)S(1)}, bf16[512,640]{0,1:T(8,128)(2,1)}, u32[]{:S(2)}) copy-start(bf16[512,640]{0,1:T(8,128)(2,1)} %copy.411) | copy-start | bytes 1966084
  382.1 4.1 %copy-start.32 = (f32[1024,128]{0,1:T(8,128)S(1)}, f32[1024,128]{0,1:T(8,128)}, u32[]{:S(2)}) copy-start(f32[1024,128]{0,1:T(8,128)} %copy-done.31) | copy-start | bytes 1572868
  (12 other events, 23.2 us)
Sparse Core Ops, SparseCore 0:
  9.7 59.4 all-gather.5
  71.4 48.6 all-gather.7
  171.7 85.9 reduce-scatter.1
  259.8 48.0 all-gather.9

commit v3 on v2

--- a/solution.py
+++ b/solution.py
@@ -202,6 +202,19 @@
     return tuple(jnp.concatenate([part[k] for part in parts], axis=1) for k in range(3))
 
 
+def gather_features(block):
+    tensor_size = lax.axis_size("tensor")
+    me = lax.axis_index("tensor")
+    arrived = [block]
+    for shift in range(1, tensor_size):
+        pairs = [(index, (index + shift) % tensor_size) for index in range(tensor_size)]
+        arrived.append(lax.ppermute(block, "tensor", pairs))
+    stacked = jnp.stack(arrived)
+    order = (me - jnp.arange(tensor_size, dtype=jnp.int32)) % tensor_size
+    ordered = jnp.take(stacked, order, axis=0)
+    return ordered.transpose(1, 0, 2).reshape(block.shape[0], tensor_size * block.shape[1])
+
+
 def layer(query, keys, values, out_weight, loss_grad, lengths, languages, labels):
     factor = 1.0 / math.sqrt(HEAD_SIZE)
     row_count = query.shape[0]
@@ -216,15 +229,19 @@
     counted = labels != -100
     lang_match = token_lang[:, None] == jnp.arange(LANGS, dtype=jnp.int32)[None, :]
     local_counts = jnp.sum((lang_match & counted[:, None]).astype(jnp.int32), axis=0)
-    padded_counts = jnp.pad(local_counts, (0, 128 - LANGS))[None, :]
-    counts = jnp.sum(lax.all_gather(padded_counts, "dp", axis=0, tiled=True), axis=0)[:LANGS].astype(
-        jnp.float32
-    )
+    dp_size = lax.axis_size("dp")
+    total_counts = local_counts
+    step = 1
+    while step < dp_size:
+        pairs = [(index, index ^ step) for index in range(dp_size)]
+        total_counts = total_counts + lax.ppermute(total_counts, "dp", pairs)
+        step *= 2
+    counts = total_counts.astype(jnp.float32)
     lang_weight = jnp.sqrt(jnp.sum(counts) / (LANGS * jnp.maximum(counts, 1.0)))
     token_weight = jnp.where(
         counted, jnp.sum(jnp.where(lang_match, lang_weight[None, :], 0.0), axis=1), 0.0
     )
-    full_grad = lax.all_gather(loss_grad, "tensor", axis=1, tiled=True)
+    full_grad = gather_features(loss_grad)
     weighted = (token_weight[:, None] * full_grad.astype(jnp.float32)).astype(jnp.bfloat16)
     out_grad = lax.dot_general(
         weighted,

time: 416 us -> 434 us (1.043)
  the two profiles are of different devices: /device:TPU:6 before, /device:TPU:0 now
where the time goes in v3:
time: 434 us; the launch traced here: 426 us
  matrix products  100 us (23%)
  waiting for transfers between devices  92.9 us (21%)
  local copies, waits for them, and re-layouts  87.4 us (20%)
  loops' own time  68.7 us (16%)
  other arithmetic  44.2 us (10%)
  between operations  17.1 us (4%)
  starting transfers between devices  15.5 us (4%)
    reduce_scatter x1, waiting for transfers between devices, layer(): lax.psum_scatter(local_term.astype(jnp.bfloat16), 'dp', scatter_dimension...  88.2 us
    another operation x2, loops' own time, cluster_backward(): lax.switch(bucket, [later_block(bucket_id) for bucket_id in range(5)], (q...  38.1 us
    unnamed x2, loops' own time  30.6 us
    unnamed x68, local copies, waits for them, and re-layouts  24.2 us
    dot_general x4, matrix products, block_forward(): jnp.einsum('grk,kd->rgd', weights, value_rows, preferred_element_type=jnp...  16.7 us
    dot_general x4, matrix products, block_backward(): jnp.einsum('rgd,kd->grk', grad_rows, value_rows, preferred_element_type=j...  16.5 us
    dot_general x4, matrix products, block_backward(): jnp.einsum('grk,rgd->kd', weights.astype(jnp.bfloat16), grad_rows, prefer...  14.9 us
    dot_general x6, matrix products, masked_scores(): jnp.einsum('rgd,kd->grk', query_rows, key_rows, preferred_element_type=jn...  12.1 us
  transfers between devices with their start and end apart: 11, of which 3 were waited for; matrix products, arithmetic and copies ran while one was open for 40% of the time, Pallas kernels for 0%

profile of v3, /device:TPU:0, one launch (start us, length us, event | category | flops | bytes accessed | tf_op | source)
XLA Modules:
  0.0 425.8 jit_solution(8829132425560876447)
XLA Ops:
  26.9 3.3 exponential_reduce_fusion.11
  50.9 20.0 %conditional.9 = (f32[5,512]{1,0:T(8,128)}, bf16[512,5,128]{2,0,1:T(8,128)(2,1)S(1)}) conditional(s32[]{:T(128)} %clamp.2, (pred[1024,1024]{0,1:T(8,128)(4,1)S(1)}, bf16[1024,128]{1,0:T(8,128)(2,1)}, bf16[512,5,128]{0,2,1:T(8,128)(2,1)}, bf16[1024,128]{1,0:T(8,128)(2,1)}) %tuple.143, ...), branch_computations={%region_22.25_spmd, %region_25.28_spmd, %region_28.31_spmd, %regio... | conditional | flops 1371338240 | bytes 35985424
  73.7 24.2 %conditional.8 = (f32[5,512]{1,0:T(8,128)}, bf16[512,5,128]{2,0,1:T(8,128)(2,1)S(1)}) conditional(s32[]{:T(128)} %clamp.2, (pred[1024,1024]{0,1:T(8,128)(4,1)S(1)}, bf16[1024,128]{1,0:T(8,128)(2,1)S(1)}, bf16[512,5,128]{0,2,1:T(8,128)(2,1)S(1)}, bf16[1024,128]{1,0:T(8,128)(2,1)S(1)}) %tuple.313, ...), branch_computations={%region_5.8_spmd, %region_8.11_spmd, %region_11.14_spmd, %region_1... | conditional | flops 1371338240 | bytes 35985424
  99.5 5.9 %pad_maximum_fusion = bf16[4,1024,640]{2,1,0:T(8,128)(2,1)} fusion(bf16[1,1024,640]{2,1,0:T(8,128)(2,1)} %bitcast.204, bf16[1,1024,640]{2,1,0:T(8,128)(2,1)} %bitcast.203, bf16[1,1024,640]{2,1,0:T(8,128)(2,1)} %bitcast.202, bf16[1,1024,640]{2,1,0:T(8,128)(2,1)} %bitcast.948), kind=kLoop, calls=%fused_computation.385 | loop fusion | flops 7864320 | bytes 10485760 | tf_op jit(solution)/shard_map/stack | solution.py:212
  105.4 6.1 %gather_fusion = bf16[4,1024,640]{2,1,0:T(8,128)(2,1)} fusion(bf16[4,1024,640]{2,1,0:T(8,128)(2,1)} %pad_maximum_fusion, s32[1024]{0:T(1024)S(1)} %pad_clamp_fusion), kind=kCustom, calls=%fused_computation | custom fusion | bytes 10485776 | tf_op jit(solution)/shard_map/jit(_take)/gather | solution.py:214
  111.4 7.2 %convert_bitcast_fusion = f32[1024,4,640]{2,0,1:T(8,128)} fusion(bf16[4,1024,640]{2,1,0:T(8,128)(2,1)} %gather_fusion, pred[4]{0:T(512)(128)(4,1)S(1)} %compare_and_fusion), kind=kLoop, calls=%fused_computation.384 | loop fusion | flops 5242880 | bytes 15728644 | tf_op jit(solution)/shard_map/convert_element_type | solution.py:245
  118.6 11.3 %copy.412 = f32[1024,4,640]{0,2,1:T(8,128)} copy(f32[1024,4,640]{2,0,1:T(8,128)} %convert_bitcast_fusion) | data formatting | bytes 20971520 | tf_op jit(solution)/shard_map/convert_element_type | solution.py:245
  129.9 7.9 %fusion.320 = bf16[1024,2560]{0,1:T(8,128)(2,1)} fusion(f32[1024,4,640]{0,2,1:T(8,128)} %copy.412, f32[1024]{0:T(1024)S(1)} %broadcast_select_fusion), kind=kLoop, calls=%fused_computation.383 | loop fusion | flops 5242880 | bytes 15732736 | tf_op jit(solution)/shard_map/convert_element_type | solution.py:245
  137.8 10.9 %convolution_convert_fusion.11 = bf16[1024,1280]{1,0:T(8,128)(2,1)S(1)} fusion(bf16[1024,2560]{0,1:T(8,128)(2,1)} %fusion.320, bf16[1280,2560]{0,1:T(8,128)(2,1)} %all-gather.3.cloned.1.call-done), kind=kOutput, calls=%fused_computation.404 | convolution fusion | flops 6712197120 | bytes 14417920 | tf_op jit(solution)/shard_map/dot_general | solution.py:246
  159.1 5.5 %multiply_reduce_fusion.10 = (f32[5,512]{1,0:T(8,128)}, bf16[5,512,128]{2,1,0:T(8,128)(2,1)S(1)}) fusion(f32[5,512,128]{2,1,0:T(8,128)} %copy.631, bf16[1024,256]{1,0:T(8,128)(2,1)} %param.30, f32[512,512,5]{1,0,2:T(8,128)} %copy-done.11, f32[5,512]{1,0:T(8,128)} %get-tuple-element.862, pred[512,512]{0,1:T(8,128)(4,1)} %copy-done.26), kind=kOutput, calls=%fused_computation.415 | convolution fusion | flops 342095360 | bytes 7628800 | tf_op jit(solution)/shard_map/grk,kd->rgd/dot_general | solution.py:34
  168.1 5.4 %multiply_reduce_fusion.11 = (f32[5,512]{1,0:T(8,128)}, bf16[5,512,128]{2,1,0:T(8,128)(2,1)S(1)}) fusion(f32[5,512,128]{2,1,0:T(8,128)} %copy.621, bf16[1024,256]{1,0:T(8,128)(2,1)} %param.30, f32[512,512,5]{1,0,2:T(8,128)} %copy-done.10, f32[5,512]{1,0:T(8,128)S(1)} %get-tuple-element.863, pred[512,512]{0,1:T(8,128)(4,1)} %copy-done.26), kind=kOutput, calls=%fused_computation.416 | convolution fusion | flops 342095360 | bytes 7622656 | tf_op jit(solution)/shard_map/grk,kd->rgd/dot_general | solution.py:34
  177.6 11.4 %convolution_convert_fusion.10 = bf16[1280,2560]{1,0:T(8,128)(2,1)} fusion(bf16[1024,2560]{0,1:T(8,128)(2,1)} %fusion.320, bf16[1024,640]{0,1:T(8,128)(2,1)} %bitcast.898, bf16[1024,640]{0,1:T(8,128)(2,1)} %bitcast.900), kind=kOutput, calls=%fused_computation.381 | convolution fusion | flops 6719406080 | bytes 14417920 | tf_op jit(solution)/shard_map/dot_general | solution.py:252
  189.1 88.2 %reduce-scatter.2.cloned.1.call-done = bf16[40,2560]{1,0:T(8,128)(2,1)} async-done(((bf16[1280,2560]{1,0:T(8,128)(2,1)}), bf16[40,2560]{1,0:T(8,128)(2,1)}) %reduce-scatter.2.cloned.1.call-update) | async-done | bytes 204816 | tf_op jit(solution)/shard_map/reduce_scatter | solution.py:255
  277.3 42.0 %conditional.10 = (f32[1024,128]{0,1:T(8,128)}, f32[1024,128]{0,1:T(8,128)}, bf16[512,640]{1,0:T(8,128)(2,1)S(1)}) conditional(s32[]{:T(128)} %clamp.2, (pred[1024,1024]{0,1:T(8,128)(4,1)}, bf16[1024,128]{1,0:T(8,128)(2,1)S(1)}, bf16[512,5,128]{0,2,1:T(8,128)(2,1)S(1)}, f32[5,512]{1,0:T(8,128)}, ...), branch_computations={%region_41.42_spmd, %region_42.43_spmd, %region_43.44_spmd, %regio... | conditional | flops 3385587200 | bytes 72020072 | solution.py:170
  296.8 3.4 fusion.185
  300.2 3.3 fusion.178
  320.1 52.2 %conditional.11 = (f32[1024,128]{0,1:T(8,128)S(1)}, f32[1024,128]{0,1:T(8,128)S(1)}, bf16[512,640]{1,0:T(8,128)(2,1)S(1)}) conditional(s32[]{:T(128)} %clamp.2, (pred[1024,1024]{0,1:T(8,128)(4,1)}, bf16[1024,128]{1,0:T(8,128)(2,1)}, bf16[512,5,128]{0,2,1:T(8,128)(2,1)}, f32[5,512]{1,0:T(8,128)}, ...), branch_computations={%region_46.47_spmd, %region_47.48_spmd, %region_48.49_spmd, %regio... | conditional | flops 3385587200 | bytes 70971472 | solution.py:170
  348.1 3.4 fusion.287
  351.6 3.6 fusion.280
  373.3 4.8 %fusion.323 = bf16[5,512,512]{1,2,0:T(8,128)(2,1)S(1)} fusion(f32[512,512,5]{1,0,2:T(8,128)} %copy-done.11, f32[5,512]{1,0:T(8,128)} %get-tuple-element.856, f32[5,512]{1,0:T(8,128)S(1)} %copy-done.57, pred[512,512]{0,1:T(8,128)(4,1)} %copy-done.26, bf16[512,5,128]{0,2,1:T(8,128)(2,1)} %bitcast.912, bf16[1024,256]{1,0:T(8,128)(2,1)} %param.30), kind=kOutput, calls=%fused_computation.389 | convolution fusion | flops 344719360 | bytes 8939520 | tf_op jit(solution)/shard_map/rgd,kd->grk/dot_general | solution.py:46
  385.1 4.8 %fusion.326 = bf16[5,512,512]{1,2,0:T(8,128)(2,1)S(1)} fusion(f32[512,512,5]{1,0,2:T(8,128)} %copy-done.10, f32[5,512]{1,0:T(8,128)} %get-tuple-element.858, f32[5,512]{1,0:T(8,128)S(1)} %copy-done.56, pred[512,512]{0,1:T(8,128)(4,1)S(1)} %copy-done.27, bf16[512,5,128]{0,2,1:T(8,128)(2,1)} %bitcast.909, bf16[1024,256]{1,0:T(8,128)(2,1)} %param.30), kind=kOutput, calls=%fused_computation.393 | convolution fusion | flops 344719360 | bytes 8939520 | tf_op jit(solution)/shard_map/rgd,kd->grk/dot_general | solution.py:46
  395.9 4.1 convolution_bitcast_fusion.10
  400.1 4.0 convolution_bitcast_fusion.11
  413.0 6.1 %copy.773 = bf16[1280,2560]{1,0:T(8,128)(2,1)} copy(bf16[1280,2560]{1,0:T(8,128)(2,1)} %all-gather.5.cloned.1.call-done) | data formatting | bytes 13107200
  (187 shorter events, 139.5 us)
Async XLA Ops:
  7.2 130.6 %all-gather.3.cloned.1.call-start = ((), (), s32[]{:S(2)}) async-start(), calls=%async_computation.1 | async-start | bytes 6758400 | tf_op jit(solution)/shard_map/all_gather | solution.py:248
  7.9 269.4 %reduce-scatter.2.cloned.1.call-start = ((), (), s32[]{:S(2)}) async-start(), calls=%async_computation.2 | async-start | bytes 6758400 | tf_op jit(solution)/shard_map/reduce_scatter | solution.py:255
  7.9 91.5 %collective-permute-start.5 = (bf16[1024,640]{1,0:T(8,128)(2,1)}, bf16[1024,640]{1,0:T(8,128)(2,1)}, u32[]{:S(2)}, u32[]{:S(2)}) collective-permute-start(bf16[1024,640]{1,0:T(8,128)(2,1)} %param.32), channel_id=1, source_target_pairs={{0,1},{1,2},{2,3},{3,0},{4,5},{5,6},{6,7},{7,4},{8,9},{9,10},{10,1... | collective-permute-start | bytes 3932168 | tf_op jit(solution)/shard_map/ppermute | solution.py:211
  10.0 89.4 %collective-permute-start.7 = (bf16[1024,640]{1,0:T(8,128)(2,1)}, bf16[1024,640]{1,0:T(8,128)(2,1)}, u32[]{:S(2)}, u32[]{:S(2)}) collective-permute-start(bf16[1024,640]{1,0:T(8,128)(2,1)} %param.32), channel_id=1, source_target_pairs={{0,3},{1,0},{2,1},{3,2},{4,7},{5,4},{6,5},{7,6},{8,11},{9,8},{10,9... | collective-permute-start | bytes 3932168 | tf_op jit(solution)/shard_map/ppermute | solution.py:211
  12.2 87.2 %collective-permute-start.6 = (bf16[1024,640]{1,0:T(8,128)(2,1)}, bf16[1024,640]{1,0:T(8,128)(2,1)}, u32[]{:S(2)}, u32[]{:S(2)}) collective-permute-start(bf16[1024,640]{1,0:T(8,128)(2,1)} %param.32), channel_id=1, source_target_pairs={{0,2},{1,3},{2,0},{3,1},{4,6},{5,7},{6,4},{7,5},{8,10},{9,11},{10,... | collective-permute-start | bytes 3932168 | tf_op jit(solution)/shard_map/ppermute | solution.py:211
  16.6 23.9 %collective-permute-start = (s32[29]{0:T(128)S(1)}, s32[29]{0:T(128)S(1)}, u32[]{:S(2)}, u32[]{:S(2)}) collective-permute-start(s32[29]{0:T(128)S(1)} %convert_reduce_fusion), channel_id=1, source_target_pairs={{0,4},{4,0},{8,12},{12,8},{16,20},{20,16},{24,28},{28,24},{32,36},... | collective-permute-start | bytes 356 | tf_op jit(solution)/shard_map/ppermute | solution.py:237
  17.8 56.0 %copy-start = (pred[1024,1024]{0,1:T(8,128)(4,1)}, pred[1024,1024]{0,1:T(8,128)(4,1)S(1)}, u32[]{:S(2)}) copy-start(pred[1024,1024]{0,1:T(8,128)(4,1)S(1)} %fusion.329) | copy-start | bytes 3145732
  17.8 12.5 %copy-start.26 = (pred[512,512]{0,1:T(8,128)(4,1)}, pred[512,512]{0,1:T(8,128)(4,1)S(1)}, u32[]{:S(2)}) copy-start(pred[512,512]{0,1:T(8,128)(4,1)S(1)} %slice.326) | copy-start | bytes 786436
  23.5 6.8 %copy-start.12 = (bf16[512,640]{0,1:T(8,128)(2,1)}, bf16[512,640]{0,1:T(8,128)(2,1)S(1)}, u32[]{:S(2)}) copy-start(bf16[512,640]{0,1:T(8,128)(2,1)S(1)} %copy.708) | copy-start | bytes 1966084
  38.4 129.7 %copy-start.55 = (f32[5,512]{1,0:T(8,128)}, f32[5,512]{1,0:T(8,128)S(1)}, u32[]{:S(2)}) copy-start(f32[5,512]{1,0:T(8,128)S(1)} %get-tuple-element.863) | copy-start | bytes 30724
  40.5 33.3 %copy-start.48 = (bf16[1024,128]{1,0:T(8,128)(2,1)}, bf16[1024,128]{1,0:T(8,128)(2,1)S(1)}, u32[]{:S(2)}) copy-start(bf16[1024,128]{1,0:T(8,128)(2,1)S(1)} %get-tuple-element.849) | copy-start | bytes 786436
  40.5 3.6 collective-permute-start.1
  44.1 5.2 %collective-permute-start.2 = (s32[29]{0:T(128)S(1)}, s32[29]{0:T(128)S(1)}, u32[]{:S(2)}, u32[]{:S(2)}) collective-permute-start(s32[29]{0:T(128)S(1)} %add.211), channel_id=1, source_target_pairs={{0,16},{4,20},{8,24},{12,28},{16,0},{20,4},{24,8},{28,12},{32,48},... | collective-permute-start | bytes 356 | tf_op jit(solution)/shard_map/ppermute | solution.py:237
  49.4 21.5 %collective-permute-start.3 = (s32[29]{0:T(128)S(1)}, s32[29]{0:T(128)S(1)}, u32[]{:S(2)}, u32[]{:S(2)}) collective-permute-start(s32[29]{0:T(128)S(1)} %add.212), channel_id=1, source_target_pairs={{0,32},{4,36},{8,40},{12,44},{16,48},{20,52},{24,56},{28,60},{32,0... | collective-permute-start | bytes 356 | tf_op jit(solution)/shard_map/ppermute | solution.py:237
  70.9 27.1 %collective-permute-start.4 = (s32[29]{0:T(128)S(1)}, s32[29]{0:T(128)S(1)}, u32[]{:S(2)}, u32[]{:S(2)}) collective-permute-start(s32[29]{0:T(128)S(1)} %add.213), channel_id=1, source_target_pairs={{0,64},{4,68},{8,72},{12,76},{16,80},{20,84},{24,88},{28,92},{32,9... | collective-permute-start | bytes 356 | tf_op jit(solution)/shard_map/ppermute | solution.py:237
  73.7 25.7 %copy-start.54 = (s32[1024]{0:T(1024)S(1)}, s32[1024]{0:T(1024)}, u32[]{:S(2)}) copy-start(s32[1024]{0:T(1024)} %param.35) | copy-start | bytes 12292
  97.9 7.4 %copy-start.8 = (bf16[512,5,128]{2,0,1:T(8,128)(2,1)}, bf16[512,5,128]{2,0,1:T(8,128)(2,1)S(1)}, u32[]{:S(2)}) copy-start(bf16[512,5,128]{2,0,1:T(8,128)(2,1)S(1)} %get-tuple-element.363) | copy-start | bytes 1966084
  189.0 224.0 %all-gather.5.cloned.1.call-start = ((), (), s32[]{:S(2)}) async-start(), calls=%async_computation.3 | async-start | bytes 6758400 | tf_op jit(solution)/shard_map/all_gather | solution.py:258
  320.1 53.2 %copy-start.57 = (f32[5,512]{1,0:T(8,128)S(1)}, f32[5,512]{1,0:T(8,128)}, u32[]{:S(2)}) copy-start(f32[5,512]{1,0:T(8,128)} %get-tuple-element.862) | copy-start | bytes 30724
  337.1 6.3 %copy-start.6 = (bf16[512,5,128]{2,0,1:T(8,128)(2,1)S(1)}, bf16[512,5,128]{2,0,1:T(8,128)(2,1)}, u32[]{:S(2)}) copy-start(bf16[512,5,128]{2,0,1:T(8,128)(2,1)} %get-tuple-element.802) | copy-start | bytes 1966084 | tf_op jit(solution)/shard_map/cond
  378.2 6.9 %copy-start.27 = (pred[512,512]{0,1:T(8,128)(4,1)S(1)}, pred[512,512]{0,1:T(8,128)(4,1)}, u32[]{:S(2)}) copy-start(pred[512,512]{0,1:T(8,128)(4,1)} %copy-done.26) | copy-start | bytes 786436
  378.2 6.9 %copy-start.56 = (f32[5,512]{1,0:T(8,128)S(1)}, f32[5,512]{1,0:T(8,128)}, u32[]{:S(2)}) copy-start(f32[5,512]{1,0:T(8,128)} %copy-done.55) | copy-start | bytes 30724
  385.1 6.3 %copy-start.28 = (f32[1024,128]{0,1:T(8,128)S(1)}, f32[1024,128]{0,1:T(8,128)}, u32[]{:S(2)}) copy-start(f32[1024,128]{0,1:T(8,128)} %get-tuple-element.815) | copy-start | bytes 1572868
  389.9 6.0 %copy-start.19 = (bf16[512,640]{0,1:T(8,128)(2,1)S(1)}, bf16[512,640]{0,1:T(8,128)(2,1)}, u32[]{:S(2)}) copy-start(bf16[512,640]{0,1:T(8,128)(2,1)} %copy.436) | copy-start | bytes 1966084
  (23 other events, 75.9 us)
Sparse Core Ops, SparseCore 0:
  10.2 51.7 all-gather.2
  189.2 88.0 reduce-scatter.1
  279.5 48.6 all-gather.4
